TPU v7x, 256 devices: a whole 4x4x8 slice. The times are simulated.
256 devices in a mesh: row: 32 (over z, x), col: 8 (over y, core).
Axes of the slice: x: 4, y: 4, z: 8, core: 2. Of those that a mesh axis runs over, the one named last changes fastest.
Arguments:
- x_points: bfloat16 [32768, 64], P(('row', 'col')), may hold values from -6 to 6
- y_points: bfloat16 [65536, 64], P(('col', 'row')), may hold values from -6 to 6
- row_mass: bfloat16 [32768], P(('row', 'col')), may hold values from 1 to 30, as said below
- col_mass: bfloat16 [65536], P(('col', 'row')), may hold values from 1 to 30, as said below
- multipliers: bfloat16 [32768, 64], P(('row', 'col')), may hold values from -12 to 12
- col_potential: bfloat16 [65536], P(('col', 'row')), may hold values from -3 to 3
- basket: float32 [64], replicated, may hold values from 0.05 to 0.25
- damping: float32 [64], replicated, may hold values from 0.3 to 1.5
Outputs:
- row_potential: float32 [32768], P('row')
- col_potential_new: float32 [65536], P('col')
- multipliers_new: float32 [32768, 64], P(('row', 'col'))
Inputs may be any that keep to these rules, and one draw needn't show every extreme that they name: `row_mass`: weights rise along the points' order by up to a factor of three. `col_mass`: weights rise along the points' order by up to a factor of three.
All inputs are finite; a program needn't handle non-finite values.
Results may differ from a plain program's by a relative error of at most 0.0012.
Values may be sent and summed in bfloat16 or wider, within the bound.
No kernel may reach another device: no remote copies, remote signals or barrier semaphores. Data moves between devices by JAX's collectives and lax.ppermute only.
A program may use at most 64 MiB of HBM per device.

v0:
```python
import jax
import jax.numpy as jnp
from jax import lax
from jax.sharding import PartitionSpec as P

EPS = 0.5
KAPPA = 0.5
RIDGE = 1.0


def joined(value, axis, join):
    pieces = jax.tree.map(lambda part: lax.all_gather(part, axis), value)
    head = jax.tree.map(lambda part: part[0], pieces)
    tail = jax.tree.map(lambda part: part[1:], pieces)
    subtotal, _ = lax.scan(lambda subtotal, piece: (join(subtotal, piece), None), head, tail)
    return subtotal


def prepare_rows(x_rows, mult_rows, basket):
    xf = x_rows.astype(jnp.float32)
    hf = mult_rows.astype(jnp.float32)
    width = xf.shape[1]
    query = hf + 2.0 * KAPPA / width * xf
    row_term = -jnp.sum(hf * xf, axis=1) - KAPPA / width * jnp.sum(xf * xf, axis=1)
    row_basket = jnp.sum(xf * basket[None, :], axis=1)
    return (query, row_term, row_basket)


def prepare_cols(y_cols, basket):
    yf = y_cols.astype(jnp.float32)
    width = yf.shape[1]
    col_term = -(KAPPA / width) * jnp.sum(yf * yf, axis=1)
    col_basket = jnp.sum(yf * basket[None, :], axis=1)
    features = jnp.concatenate([yf, yf * yf], axis=1).astype(jnp.bfloat16)
    return (yf, col_term, col_basket, features)


def scores(query, row_term, row_basket, y_float, col_term, col_basket):
    dots = lax.dot_general(
        query,
        y_float,
        (((1,), (1,)), ((), ())),
        precision=lax.Precision.HIGHEST,
        preferred_element_type=jnp.float32,
    )
    payoff = jax.nn.relu(col_basket[None, :] - row_basket[:, None])
    return (dots + row_term[:, None] + col_term[None, :] + payoff) / EPS


def lse_join(first, second):
    top = jnp.maximum(first[0], second[0])
    total = first[1] * jnp.exp(first[0] - top) + second[1] * jnp.exp(second[0] - top)
    return (top, total)


def on_device(x_points, y_points, row_mass, col_mass, multipliers, col_potential, basket, damping):
    x_rows, mult_rows, mass_rows = (
        lax.all_gather(x_points, "col", axis=0, tiled=True),
        lax.all_gather(multipliers, "col", axis=0, tiled=True),
        lax.all_gather(row_mass, "col", axis=0, tiled=True),
    )
    y_cols, pot_cols, mass_cols = (
        lax.all_gather(y_points, "row", axis=0, tiled=True),
        lax.all_gather(col_potential, "row", axis=0, tiled=True),
        lax.all_gather(col_mass, "row", axis=0, tiled=True),
    )
    query, row_term, row_basket = prepare_rows(x_rows, mult_rows, basket)
    y_float, col_term, col_basket, features = prepare_cols(y_cols, basket)
    row_weight = mass_rows.astype(jnp.float32)
    col_weight = mass_cols.astype(jnp.float32)
    log_row = jnp.log(row_weight)
    log_col = jnp.log(col_weight)
    nrows = x_rows.shape[0]
    block = min(128, nrows)
    count = nrows // block
    starts = jnp.arange(count, dtype=jnp.int32) * block

    def cut(arr, start):
        return lax.dynamic_slice_in_dim(arr, start, block, 0)

    def block_scores(start):
        return scores(
            cut(query, start),
            cut(row_term, start),
            cut(row_basket, start),
            y_float,
            col_term,
            col_basket,
        )

    gshift = pot_cols.astype(jnp.float32) / EPS + log_col

    def row_pass(start):
        z = block_scores(start) + gshift[None, :]
        top = jnp.max(z, axis=1)
        total = jnp.sum(jnp.exp(z - top[:, None]), axis=1)
        return (top, total)

    row_tops, row_totals = lax.map(row_pass, starts)
    row_tops = row_tops.reshape(nrows)
    row_totals = row_totals.reshape(nrows)
    mu_total, nu_total = lax.psum(
        (jnp.sum(row_mass.astype(jnp.float32)), jnp.sum(col_mass.astype(jnp.float32))),
        ("row", "col"),
    )
    row_top, row_total = joined((row_tops, row_totals), "col", lse_join)
    log_nu_total = jnp.log(nu_total)
    row_potential = -EPS * (row_top + jnp.log(row_total) - log_nu_total)
    fshift = row_potential / EPS + log_row

    def col_pass(start):
        z = block_scores(start) + cut(fshift, start)[:, None]
        top = jnp.max(z, axis=0)
        total = jnp.sum(jnp.exp(z - top[None, :]), axis=0)
        return (top, total)

    col_tops, col_totals = lax.map(col_pass, starts)
    col_top = jnp.max(col_tops, axis=0)
    col_total = jnp.sum(col_totals * jnp.exp(col_tops - col_top[None, :]), axis=0)
    peak = lax.pmax(col_top, "row")
    scaled = col_total * jnp.exp(col_top - peak)
    whole = lax.psum(scaled, "row")
    col_potential_new = -EPS * (peak + jnp.log(whole) - jnp.log(mu_total))
    gq = col_potential_new / EPS + log_col - log_nu_total
    fq = row_potential / EPS

    def moment_pass(start):
        plan = jnp.exp(block_scores(start) + cut(fq, start)[:, None] + gq[None, :]).astype(
            jnp.bfloat16
        )
        both = jnp.dot(plan, features, preferred_element_type=jnp.float32)
        mass = jnp.sum(plan.astype(jnp.float32), axis=1)
        return (both, mass)

    both, mass = lax.map(moment_pass, starts)
    both = both.reshape(nrows, features.shape[1])
    mass = mass.reshape(nrows)
    share = x_points.shape[0]
    both_all, mass_all = lax.psum((both, mass), "col")
    offset = lax.axis_index("col") * share
    own_both = lax.dynamic_slice_in_dim(both_all, offset, share, 0)
    own_mass = lax.dynamic_slice_in_dim(mass_all, offset, share, 0)
    width = x_points.shape[1]
    first = own_both[:, :width]
    second = own_both[:, width:]
    xf = x_points.astype(jnp.float32)
    grad = first - xf * own_mass[:, None]
    curv = (second - 2.0 * xf * first + xf * xf * own_mass[:, None]) / EPS + RIDGE
    multipliers_new = multipliers.astype(jnp.float32) - damping[None, :] * grad / curv
    return (row_potential, col_potential_new, multipliers_new)


def solution(mesh):
    placed = (
        P(("row", "col"), None),
        P(("col", "row"), None),
        P(("row", "col")),
        P(("col", "row")),
        P(("row", "col"), None),
        P(("col", "row")),
        P(),
        P(),
    )
    return jax.shard_map(
        on_device,
        mesh=mesh,
        in_specs=placed,
        out_specs=(P("row"), P("col"), P(("row", "col"), None)),
        check_vma=False,
    )
```

profile of v0, /device:TPU:2, one launch (start us, length us, event | category | flops | bytes accessed | tf_op | source)
XLA Modules:
  0.0 851.1 jit_solution(13461661143674850518)
XLA Ops:
  11.3 79.4 %all-reduce = (f32[]{:T(128)}, f32[]{:T(128)}) all-reduce(f32[]{:T(128)} %convert_reduce_fusion.1, f32[]{:T(128)} %convert_reduce_fusion.2), channel_id=1, replica_groups=mesh['row'=32,'col'=8] {'row','col'}, use_global_device_ids=true, to_apply=%region_12.13 | all-reduce | flops 2 | bytes 16 | tf_op jit(solution)/shard_map/psum | solution.py:102
  95.0 42.6 %all-gather.1 = bf16[32,1,256]{2,1,0:T(2,128)(2,1)S(1)} all-gather(bf16[1,1,256]{2,1,0:T(2,128)(2,1)S(1)} %reshape.38), channel_id=1, replica_groups=mesh['row'=32,'col'=8] {'row'}, dimensions={0}, use_global_device_ids=true | all-gather | bytes 16896 | tf_op jit(solution)/shard_map/all_gather | solution.py:65
  137.6 40.5 %all-gather = bf16[32,1,256]{2,1,0:T(2,128)(2,1)S(1)} all-gather(bf16[1,1,256]{2,1,0:T(2,128)(2,1)S(1)} %reshape.36), channel_id=1, replica_groups=mesh['row'=32,'col'=8] {'row'}, dimensions={0}, use_global_device_ids=true | all-gather | bytes 16896 | tf_op jit(solution)/shard_map/all_gather | solution.py:64
  178.2 9.2 %all-gather.4 = bf16[8,1,128]{2,1,0:T(2,128)(2,1)S(1)} all-gather(bf16[1,1,128]{2,1,0:T(2,128)(2,1)} %bitcast.86), channel_id=1, replica_groups=mesh['row'=32,'col'=8] {'col'}, dimensions={0}, use_global_device_ids=true | all-gather | bytes 2304 | tf_op jit(solution)/shard_map/all_gather | solution.py:60
  187.4 12.8 %all_gather.24 = bf16[1024,64]{1,0:T(8,128)(2,1)S(1)} all-gather(bf16[128,64]{1,0:T(8,128)(2,1)S(1)} %copy.15), channel_id=1, replica_groups=mesh['row'=32,'col'=8] {'col'}, dimensions={0}, use_global_device_ids=true | all-gather | bytes 147456 | tf_op jit(solution)/shard_map/all_gather | solution.py:59
  200.2 12.8 %all_gather.25 = bf16[1024,64]{1,0:T(8,128)(2,1)S(1)} all-gather(bf16[128,64]{1,0:T(8,128)(2,1)S(1)} %copy.16), channel_id=1, replica_groups=mesh['row'=32,'col'=8] {'col'}, dimensions={0}, use_global_device_ids=true | all-gather | bytes 147456 | tf_op jit(solution)/shard_map/all_gather | solution.py:58
  221.7 80.0 %while.48 = (s32[]{:T(128)}, f32[8,128]{1,0:T(8,128)S(1)}, f32[8,128]{1,0:T(8,128)S(1)}, s32[8]{0:T(128)S(1)}, f32[1024,64]{1,0:T(8,128)S(1)}, /*index=5*/f32[81...) while((s32[]{:T(128)}, f32[8,128]{1,0:T(8,128)S(1)}, ...), condition=%wide.region_8.9_spmd, body=%wide.region_5.8_spmd.sunk | while | flops 815791872 | bytes 10656463 | solution.py:99
  224.4 6.5 fusion.52
  234.4 6.5 fusion.52
  244.4 6.5 fusion.52
  254.4 6.5 fusion.52
  264.4 6.5 fusion.52
  274.4 6.5 fusion.52
  284.4 6.5 fusion.52
  294.4 6.5 fusion.52
  301.7 12.9 %all-gather.2 = f32[8,1,1024]{2,1,0:T(1,128)S(1)} all-gather(f32[1,1,1024]{2,1,0:T(1,128)S(1)} %bitcast.83), channel_id=1, replica_groups=mesh['row'=32,'col'=8] {'col'}, dimensions={0}, use_global_device_ids=true | all-gather | bytes 36864 | tf_op jit(solution)/shard_map/all_gather | solution.py:12
  314.7 13.1 %all-gather.3 = f32[8,1,1024]{2,1,0:T(1,128)S(1)} all-gather(f32[1,1,1024]{2,1,0:T(1,128)S(1)} %bitcast.82), channel_id=1, replica_groups=mesh['row'=32,'col'=8] {'col'}, dimensions={0}, use_global_device_ids=true | all-gather | bytes 36864 | tf_op jit(solution)/shard_map/all_gather | solution.py:12
  328.7 80.8 %while.50 = (s32[]{:T(128)}, f32[8,8192]{1,0:T(8,128)S(1)}, f32[8,8192]{1,0:T(8,128)S(1)}, s32[8]{0:T(128)S(1)}, f32[1024,64]{1,0:T(8,128)S(1)}, /*index=5*/f32[...) while((s32[]{:T(128)}, f32[8,8192]{1,0:T(8,128)S(1)}, ...), condition=%wide.region_16.17_spmd, body=%wide.region_13.16_spmd.sunk | while | flops 815775744 | bytes 10851027 | solution.py:117
  331.5 6.4 fusion.54
  409.7 136.0 %pmax.7 = f32[8192]{0:T(1024)S(1)} all-reduce(f32[8192]{0:T(1024)S(1)} %reduce_max.27), channel_id=1, replica_groups=mesh['row'=32,'col'=8] {'row'}, use_global_device_ids=true, to_apply=%region_18.19 | all-reduce | flops 8192 | bytes 65536 | tf_op jit(solution)/shard_map/pmax | solution.py:120
  545.8 139.9 %psum.36 = f32[8192]{0:T(1024)S(1)} all-reduce(f32[8192]{0:T(1024)S(1)} %exponential_multiply_fusion), channel_id=1, replica_groups=mesh['row'=32,'col'=8] {'row'}, use_global_device_ids=true, to_apply=%region_20.21 | all-reduce | flops 8192 | bytes 65536 | tf_op jit(solution)/shard_map/psum | solution.py:122
  689.8 88.4 %while.51 = (s32[]{:T(128)}, f32[8,128,128]{2,1,0:T(8,128)S(1)}, f32[8,128]{1,0:T(8,128)S(1)}, s32[8]{0:T(128)S(1)}, f32[1024,64]{1,0:T(8,128)S(1)}, /*index=5*/...) while((s32[]{:T(128)}, f32[8,128,128]{2,1,0:T(8,128)S(1)}, ...), condition=%wide.region_25.26_spmd, body=%wide.region_23.25_spmd.sunk | while | flops 1085276032 | bytes 8624355 | solution.py:135
  692.5 7.5 convert_reduce_fusion.4
  703.6 7.5 convert_reduce_fusion.4
  714.6 7.5 convert_reduce_fusion.4
  725.7 7.5 convert_reduce_fusion.4
  736.7 7.5 convert_reduce_fusion.4
  747.8 7.5 convert_reduce_fusion.4
  758.8 7.5 convert_reduce_fusion.4
  769.9 7.5 convert_reduce_fusion.4
  779.2 12.4 %psum.39 = f32[1024]{0:T(1024)S(1)} all-reduce(f32[1024]{0:T(1024)S(1)} %bitcast.84), channel_id=1, replica_groups=mesh['row'=32,'col'=8] {'col'}, use_global_device_ids=true, to_apply=%region_27.28 | all-reduce | flops 1024 | bytes 8192 | tf_op jit(solution)/shard_map/psum | solution.py:139
  791.7 51.1 %all-reduce.3.cloned.1.call-done = f32[1024,128]{0,1:T(8,128)} async-done(((f32[1024,128]{0,1:T(8,128)}), f32[1024,128]{0,1:T(8,128)}) %all-reduce.3.cloned.1.call-update) | async-done | bytes 524304 | tf_op jit(solution)/shard_map/psum | solution.py:139
  (225 shorter events, 107.6 us)
Async XLA Ops:
  7.2 207.1 %all-gather.7.cloned.1.call-start = ((), (), s32[]{:S(2)}) async-start(), calls=%async_computation | async-start | bytes 2162688 | tf_op jit(solution)/shard_map/all_gather | solution.py:63
  8.7 834.1 %all-reduce.3.cloned.1.call-start = ((), (), s32[]{:S(2)}) async-start(), calls=%async_computation.1 | async-start | bytes 1048576 | tf_op jit(solution)/shard_map/psum | solution.py:139
  214.3 5.2 copy-start
  689.7 153.1 %copy-start.1 = (bf16[128,64]{0,1:T(8,128)(2,1)S(1)}, bf16[128,64]{0,1:T(8,128)(2,1)}, u32[]{:S(2)}) copy-start(bf16[128,64]{0,1:T(8,128)(2,1)} %param.16) | copy-start | bytes 49156
  689.7 153.1 %copy-start.2 = (bf16[128,64]{0,1:T(8,128)(2,1)S(1)}, bf16[128,64]{0,1:T(8,128)(2,1)}, u32[]{:S(2)}) copy-start(bf16[128,64]{0,1:T(8,128)(2,1)} %param.20) | copy-start | bytes 49156
  689.8 153.1 %copy-start.3 = (f32[64]{0:T(128)S(1)}, f32[64]{0:T(128)}, u32[]{:S(2)}) copy-start(f32[64]{0:T(128)} %param.23) | copy-start | bytes 772
Sparse Core Ops, SparseCore 0:
  10.6 79.5 all-gather.6
  779.3 63.4 all-reduce.2
where the time goes:
time: 853 us; the launch traced here: 851 us
  blocking collectives  512 us (60%)
  matrix products  169 us (20%)
  waiting for transfers between devices  51.2 us (6%)
  loops' own time  47.5 us (6%)
  other arithmetic  28.6 us (3%)
  local copies, waits for them, and re-layouts  27.8 us (3%)
  between operations  15.6 us (2%)
    dot_general x24, matrix products, scores(): lax.dot_general(query, y_float, (((1,), (1,)), ((), ())), precision=lax.P...  163 us
    psum x1, blocking collectives, on_device(): whole = lax.psum(scaled, 'row')  140 us
    pmax x1, blocking collectives, on_device(): peak = lax.pmax(col_top, 'row')  136 us
    psum x1, blocking collectives, on_device(): lax.psum((jnp.sum(row_mass.astype(jnp.float32)), jnp.sum(col_mass.astype(...  79.4 us
    psum x1, waiting for transfers between devices, on_device(): both_all, mass_all = lax.psum((both, mass), 'col')  51.1 us
    all_gather x1, blocking collectives, on_device(): lax.all_gather(col_mass, 'row', axis=0, tiled=True)  42.6 us
    all_gather x1, blocking collectives, on_device(): lax.all_gather(col_potential, 'row', axis=0, tiled=True)  40.5 us
    all_gather x2, blocking collectives, joined(): pieces = jax.tree.map(lambda part: lax.all_gather(part, axis), value)  26 us
  transfers between devices with their start and end apart: 2, of which 1 were waited for; matrix products, arithmetic and copies ran while one was open for 1% of the time, Pallas kernels for 0%

commit v1 on v0

v1 whole, which is shorter than its diff:
```python
import jax
import jax.numpy as jnp
from jax import lax
from jax.sharding import PartitionSpec as P

EPS = 0.5
KAPPA = 0.5
RIDGE = 1.0


def merge_lse(parts):
    top = jnp.max(parts, axis=0)
    return top + jnp.log(jnp.sum(jnp.exp(parts - top[None, :]), axis=0))


def on_device(x_points, y_points, row_mass, col_mass, multipliers, col_potential, basket, damping):
    width = x_points.shape[1]
    share = x_points.shape[0]
    x_pack = jnp.concatenate([x_points, multipliers, row_mass[:, None]], axis=1)
    x_rows_pack = lax.all_gather(x_pack, "col", axis=0, tiled=True)
    x_rows = x_rows_pack[:, :width]
    mult_rows = x_rows_pack[:, width : 2 * width]
    mass_rows = x_rows_pack[:, 2 * width]
    ny = y_points.shape[0]
    own_rmass = jnp.zeros((ny,), jnp.bfloat16).at[:share].set(row_mass)
    y_pack = jnp.concatenate(
        [y_points, col_potential[:, None], col_mass[:, None], own_rmass[:, None]], axis=1
    )
    y_cols_pack = lax.all_gather(y_pack, "row", axis=0, tiled=True)
    y_cols = y_cols_pack[:, :width]
    pot_cols = y_cols_pack[:, width].astype(jnp.float32)
    mass_cols = y_cols_pack[:, width + 1].astype(jnp.float32)
    rmass_part = jnp.sum(y_cols_pack[:, width + 2].astype(jnp.float32))

    xf = x_rows.astype(jnp.float32)
    hf = mult_rows.astype(jnp.float32)
    yf = y_cols.astype(jnp.float32)
    row_term2 = 2.0 * (-jnp.sum(hf * xf, axis=1) - KAPPA / width * jnp.sum(xf * xf, axis=1))
    row_basket2 = 2.0 * jnp.sum(xf * basket[None, :], axis=1)
    col_term2 = 2.0 * (-(KAPPA / width) * jnp.sum(yf * yf, axis=1))
    col_basket2 = 2.0 * jnp.sum(yf * basket[None, :], axis=1)
    q_aug = jnp.concatenate([mult_rows * 2, x_rows * (2.0 * KAPPA / width * 2.0)], axis=1)
    y_aug = jnp.concatenate([y_cols, y_cols], axis=1)
    features = jnp.concatenate([yf, yf * yf], axis=1).astype(jnp.bfloat16)

    row_weight = mass_rows.astype(jnp.float32)
    log_row = jnp.log(row_weight)
    log_col = jnp.log(mass_cols)
    nrows = x_rows.shape[0]
    block = min(128, nrows)
    count = nrows // block
    starts = jnp.arange(count, dtype=jnp.int32) * block

    def cut(arr, start):
        return lax.dynamic_slice_in_dim(arr, start, block, 0)

    def block_z(start, row_bias, col_bias):
        dots = jnp.dot(cut(q_aug, start), y_aug.T, preferred_element_type=jnp.float32)
        payoff = jnp.maximum(col_basket2[None, :] - cut(row_basket2, start)[:, None], 0.0)
        return dots + cut(row_bias, start)[:, None] + col_bias[None, :] + payoff

    gshift = col_term2 + pot_cols / EPS + log_col
    zero_rows = jnp.zeros((nrows,), jnp.float32)

    def row_pass(start):
        z = block_z(start, row_term2, gshift)
        top = jnp.max(z, axis=1)
        total = jnp.sum(jnp.exp(z - top[:, None]), axis=1)
        return top + jnp.log(total)

    row_local = lax.map(row_pass, starts).reshape(nrows)
    nu_part = jnp.sum(mass_cols)
    row_msg = jnp.concatenate([row_local, jnp.stack([nu_part, rmass_part])])
    row_all = lax.all_gather(row_msg, "col", axis=0)
    nu_total = jnp.sum(row_all[:, nrows])
    mu_total = jnp.sum(row_all[:, nrows + 1])
    log_nu_total = jnp.log(nu_total)
    row_potential = -EPS * (merge_lse(row_all[:, :nrows]) - log_nu_total)
    fshift = row_term2 + row_potential / EPS + log_row
    zero_cols = jnp.zeros_like(gshift)

    def col_pass(start):
        z = block_z(start, fshift, col_term2)
        top = jnp.max(z, axis=0)
        total = jnp.sum(jnp.exp(z - top[None, :]), axis=0)
        return (top, total)

    col_tops, col_totals = lax.map(col_pass, starts)
    col_top = jnp.max(col_tops, axis=0)
    col_total = jnp.sum(col_totals * jnp.exp(col_tops - col_top[None, :]), axis=0)
    col_local = col_top + jnp.log(col_total)
    col_all = lax.all_gather(col_local, "row", axis=0)
    col_potential_new = -EPS * (merge_lse(col_all) - jnp.log(mu_total))
    gq = col_term2 + col_potential_new / EPS + log_col - log_nu_total
    fq = row_term2 + row_potential / EPS

    def moment_pass(start):
        plan = jnp.exp(block_z(start, fq, gq)).astype(jnp.bfloat16)
        both = jnp.dot(plan, features, preferred_element_type=jnp.float32)
        mass = jnp.sum(plan.astype(jnp.float32), axis=1)
        return jnp.concatenate([both, mass[:, None]], axis=1)

    both = lax.map(moment_pass, starts).reshape(nrows, 2 * width + 1)
    own = lax.psum_scatter(both, "col", scatter_dimension=0, tiled=True)
    first = own[:, :width]
    second = own[:, width : 2 * width]
    own_mass = own[:, 2 * width]
    xo = x_points.astype(jnp.float32)
    grad = first - xo * own_mass[:, None]
    curv = (second - 2.0 * xo * first + xo * xo * own_mass[:, None]) / EPS + RIDGE
    multipliers_new = multipliers.astype(jnp.float32) - damping[None, :] * grad / curv
    return (row_potential, col_potential_new, multipliers_new)


def solution(mesh):
    placed = (
        P(("row", "col"), None),
        P(("col", "row"), None),
        P(("row", "col")),
        P(("col", "row")),
        P(("row", "col"), None),
        P(("col", "row")),
        P(),
        P(),
    )
    return jax.shard_map(
        on_device,
        mesh=mesh,
        in_specs=placed,
        out_specs=(P("row"), P("col"), P(("row", "col"), None)),
        check_vma=False,
    )
```

time: 853 us -> 435 us (0.51)
  blocking collectives: 512 us -> 37.7 us
  waiting for transfers between devices: 51.2 us -> 164 us
  matrix products: 169 us -> 77.7 us
  local copies, waits for them, and re-layouts: 27.8 us -> 59.4 us
    psum x3 -> x0, blocking collectives: 232 us -> none  [the longest x1 140 us: on_device(): whole = lax.psum(scaled, 'row')]
    pmax x1 -> x0, blocking collectives: 136 us -> none  [on_device(): peak = lax.pmax(col_top, 'row')]
    all_gather x1 -> x2, waiting for transfers between devices: 0.02 us -> 131 us  [the longest x1 70.7 us: on_device(): col_all = lax.all_gather(col_local, 'row', axis=0)]
    all_gather x7 -> x1, blocking collectives: 144 us -> 13.6 us  [on_device(): x_rows_pack = lax.all_gather(x_pack, 'col', axis=0, tiled=True)]
    dot_general x24, matrix products: 163 us -> 69.9 us  [block_z(): jnp.dot(cut(q_aug, start), y_aug.T, preferred_element_type=jnp.float32)]
    psum x1 -> x0, waiting for transfers between devices: 51.1 us -> none  [on_device(): both_all, mass_all = lax.psum((both, mass), 'col')]
    reduce_scatter x0 -> x1, waiting for transfers between devices: none -> 32.8 us  [on_device(): own = lax.psum_scatter(both, 'col', scatter_dimension=0, tiled=True)]
    dynamic_update_slice x24, local copies, waits for them, and re-layouts: 0.83 us -> 27.3 us  [the longest x16 27.1 us: on_device(): both = lax.map(moment_pass, starts).reshape(nrows, 2 * width + 1)]
  transfers between devices with their start and end apart: 2 -> 3, of which waited for: 1 -> 3; matrix products, arithmetic and copies ran while one was open for 1% -> 1% of each run, Pallas kernels for 0% -> 0%
where the time goes in v1:
time: 435 us; the launch traced here: 432 us
  waiting for transfers between devices  164 us (38%)
  matrix products  77.7 us (18%)
  local copies, waits for them, and re-layouts  59.4 us (14%)
  loops' own time  46.6 us (11%)
  blocking collectives  37.7 us (9%)
  other arithmetic  30.7 us (7%)
  between operations  16 us (4%)
    all_gather x1, waiting for transfers between devices, on_device(): col_all = lax.all_gather(col_local, 'row', axis=0)  70.7 us
    dot_general x24, matrix products, block_z(): jnp.dot(cut(q_aug, start), y_aug.T, preferred_element_type=jnp.float32)  69.9 us
    all_gather x1, waiting for transfers between devices, on_device(): y_cols_pack = lax.all_gather(y_pack, 'row', axis=0, tiled=True)  60.6 us
    reduce_scatter x1, waiting for transfers between devices, on_device(): own = lax.psum_scatter(both, 'col', scatter_dimension=0, tiled=True)  32.8 us
    dynamic_update_slice x16, local copies, waits for them, and re-layouts, on_device(): both = lax.map(moment_pass, starts).reshape(nrows, 2 * width + 1)  27.1 us
    unnamed x1, blocking collectives  24.1 us
    another operation x1, loops' own time, on_device(): col_tops, col_totals = lax.map(col_pass, starts)  15.8 us
    another operation x1, loops' own time, on_device(): both = lax.map(moment_pass, starts).reshape(nrows, 2 * width + 1)  15.8 us
  transfers between devices with their start and end apart: 3, of which 3 were waited for; matrix products, arithmetic and copies ran while one was open for 1% of the time, Pallas kernels for 0%

profile of v1, /device:TPU:2, one launch (start us, length us, event | category | flops | bytes accessed | tf_op | source)
XLA Modules:
  0.0 432.2 jit_solution(2858686389016648679)
XLA Ops:
  14.9 13.6 %all_gather.16 = bf16[1024,129]{1,0:T(8,128)(2,1)S(1)} all-gather(bf16[128,129]{1,0:T(8,128)(2,1)S(1)} %pad_maximum_fusion.3), channel_id=1, replica_groups=mesh['row'=32,'col'=8] {'col'}, dimensions={0}, use_global_device_ids=true | all-gather | bytes 297216 | tf_op jit(solution)/shard_map/all_gather | solution.py:20
  30.3 60.6 %all-gather.5.cloned.1.call-done = bf16[8192,67]{1,0:T(8,128)(2,1)} async-done(((bf16[256,67]{1,0:T(8,128)(2,1)}), bf16[8192,67]{1,0:T(8,128)(2,1)}) %all-gather.5.cloned.1.call-update) | async-done | bytes 1097744 | tf_op jit(solution)/shard_map/all_gather | solution.py:29
  90.9 4.0 fusion.16
  94.9 3.4 pad_maximum_fusion.1
  98.3 5.0 %convert_reduce_fusion.2 = (f32[]{:T(128)}, f32[]{:T(128)}, f32[8192]{0:T(1024)S(1)}, f32[8192]{0:T(1024)S(1)}) fusion(bf16[8192,67]{1,0:T(8,128)(2,1)S(1)} %copy-done), kind=kLoop, calls=%fused_computation.30 | loop fusion | flops 49150 | bytes 114696 | tf_op jit(solution)/shard_map/reduce_sum | solution.py:33
  103.3 49.9 %while.33 = (s32[]{:T(128)}, f32[8,128]{1,0:T(8,128)S(1)}, s32[8]{0:T(128)S(1)}, bf16[1024,128]{1,0:T(8,128)(2,1)S(1)}, bf16[8192,128]{1,0:T(8,128)(2,1)}, /*ind...) while((s32[]{:T(128)}, f32[8,128]{1,0:T(8,128)S(1)}, ...), condition=%wide.region_8.0_spmd, body=%wide.region_5.8_spmd.sunk | while | flops 276823936 | bytes 10591411 | solution.py:71
  118.4 2.8 fusion.51
  124.6 2.8 fusion.51
  130.9 2.8 fusion.51
  137.1 2.8 fusion.51
  143.3 2.8 fusion.51
  154.9 24.1 %all-reduce.1 = f32[8208]{0:T(1024)S(1)} all-reduce(f32[8208]{0:T(1024)S(1)} %dynamic-update-slice.3), channel_id=2, replica_groups=mesh['row'=32,'col'=8] {'col'}, use_global_device_ids=true, to_apply=%add.1 | all-reduce | flops 8208 | bytes 65664
  181.1 51.2 %while.34 = (s32[]{:T(128)}, f32[8,8192]{1,0:T(8,128)S(1)}, f32[8,8192]{1,0:T(8,128)S(1)}, s32[8]{0:T(128)S(1)}, bf16[1024,128]{1,0:T(8,128)(2,1)S(1)}, /*index=...) while((s32[]{:T(128)}, f32[8,8192]{1,0:T(8,128)S(1)}, ...), condition=%wide.region_17.18_spmd, body=%wide.region_14.0_spmd.sunk | while | flops 276807680 | bytes 10816703 | solution.py:88
  233.8 70.7 %all-gather.7.cloned.1.call-done = f32[262144]{0:T(1024)} async-done(((f32[8192]{0:T(1024)}), f32[262144]{0:T(1024)}) %all-gather.7.cloned.1.call-update) | async-done | bytes 1048592 | tf_op jit(solution)/shard_map/all_gather | solution.py:92
  306.9 81.9 %while.35 = (s32[]{:T(128)}, f32[8,128,129]{1,0,2:T(8,128)}, s32[8]{0:T(128)S(1)}, bf16[1024,128]{1,0:T(8,128)(2,1)S(1)}, bf16[8192,128]{1,0:T(8,128)(2,1)}, /*i...) while((s32[]{:T(128)}, f32[8,128,129]{1,0,2:T(8,128)}, ...), condition=%wide.region_25.26_spmd, body=%wide.region_23.25_spmd.sunk | while | flops 545275904 | bytes 8952507 | solution.py:103
  309.6 3.2 convert_reduce_fusion.4
  313.8 3.3 dynamic_update_slice.22
  319.8 3.2 convert_reduce_fusion.4
  324.1 3.3 dynamic_update_slice.22
  330.0 3.2 convert_reduce_fusion.4
  334.3 3.3 dynamic_update_slice.22
  340.3 3.2 convert_reduce_fusion.4
  344.5 3.3 dynamic_update_slice.22
  350.5 3.2 convert_reduce_fusion.4
  354.8 3.3 dynamic_update_slice.22
  360.8 3.2 convert_reduce_fusion.4
  365.0 3.3 dynamic_update_slice.22
  371.0 3.2 convert_reduce_fusion.4
  375.3 3.3 dynamic_update_slice.22
  381.2 3.2 convert_reduce_fusion.4
  385.5 3.3 dynamic_update_slice.22
  390.8 32.8 %reduce-scatter.2.cloned.1.call-done = f32[128,129]{0,1:T(8,128)} async-done(((f32[1024,129]{0,1:T(8,128)}), f32[128,129]{0,1:T(8,128)}) %reduce-scatter.2.cloned.1.call-update) | async-done | bytes 66064 | tf_op jit(solution)/shard_map/reduce_scatter | solution.py:104
  (209 shorter events, 89.6 us)
Async XLA Ops:
  7.2 83.7 %all-gather.5.cloned.1.call-start = ((), (), s32[]{:S(2)}) async-start(), calls=%async_computation.1 | async-start | bytes 2162688 | tf_op jit(solution)/shard_map/all_gather | solution.py:29
  11.2 293.4 %all-gather.7.cloned.1.call-start = ((), (), s32[]{:S(2)}) async-start(), calls=%async_computation.3 | async-start | bytes 1081344 | tf_op jit(solution)/shard_map/all_gather | solution.py:92
  90.9 4.0 copy-start
  233.1 190.5 %reduce-scatter.2.cloned.1.call-start = ((), (), s32[]{:S(2)}) async-start(), calls=%async_computation.2 | async-start | bytes 626688 | tf_op jit(solution)/shard_map/reduce_scatter | solution.py:104
  306.9 117.4 %copy-start.1 = (bf16[128,64]{0,1:T(8,128)(2,1)S(1)}, bf16[128,64]{0,1:T(8,128)(2,1)}, u32[]{:S(2)}) copy-start(bf16[128,64]{0,1:T(8,128)(2,1)} %param.20) | copy-start | bytes 49156
  306.9 117.4 %copy-start.2 = (bf16[128,64]{0,1:T(8,128)(2,1)S(1)}, bf16[128,64]{0,1:T(8,128)(2,1)}, u32[]{:S(2)}) copy-start(bf16[128,64]{0,1:T(8,128)(2,1)} %param.16) | copy-start | bytes 49156
  306.9 117.4 %copy-start.3 = (f32[64]{0:T(128)S(1)}, f32[64]{0:T(128)}, u32[]{:S(2)}) copy-start(f32[64]{0:T(128)} %param.23) | copy-start | bytes 772
Sparse Core Ops, SparseCore 0:
  11.3 79.5 all-gather.4
  233.2 71.2 all-gather.6
  390.9 32.5 reduce-scatter.1

commit v2 on v1

v2 whole, which is shorter than its diff:
```python
import functools

import jax
import jax.numpy as jnp
from jax import lax
from jax.experimental import pallas as pl
from jax.sharding import Mesh, PartitionSpec as P

EPS = 0.5
KAPPA = 0.5
RIDGE = 1.0


ROW = ("z", "x")
COL = ("y", "core")


def gather_row(value):
    inner = lax.all_gather(value, ROW[1], axis=0, tiled=True)
    return lax.all_gather(inner, ROW[0], axis=0, tiled=True)


def gather_col(value):
    return lax.all_gather(value, COL, axis=0, tiled=True)


KF = 256
INTERPRET = False


def _row_lse_kernel(qa_ref, yat_ref, rb_ref, cb_ref, ra_ref, ca_ref, out_ref, *, tn):
    tm = qa_ref.shape[0]
    n = yat_ref.shape[1]
    qa = qa_ref[...]
    rb = rb_ref[...]
    ra = ra_ref[...]

    def body(k, carry):
        m, l = carry
        j = pl.multiple_of(k * tn, tn)
        s = jnp.dot(qa, yat_ref[:, pl.ds(j, tn)], preferred_element_type=jnp.float32)
        z = s + ra + ca_ref[:, pl.ds(j, tn)] + jnp.maximum(cb_ref[:, pl.ds(j, tn)] - rb, 0.0)
        m_new = jnp.maximum(m, jnp.max(z, axis=1, keepdims=True))
        l = l * jnp.exp(m - m_new) + jnp.sum(jnp.exp(z - m_new), axis=1, keepdims=True)
        return m_new, l

    m0 = jnp.full((tm, 1), -jnp.inf, jnp.float32)
    l0 = jnp.zeros((tm, 1), jnp.float32)
    m, l = lax.fori_loop(0, n // tn, body, (m0, l0))
    out_ref[...] = m + jnp.log(l)


def row_lse(qa, yat, rb, cb, ra, ca, tm=128, tn=512):
    nr, kq = qa.shape
    n = yat.shape[1]
    return pl.pallas_call(
        functools.partial(_row_lse_kernel, tn=tn),
        grid=(nr // tm,),
        in_specs=[
            pl.BlockSpec((tm, kq), lambda i: (i, 0)),
            pl.BlockSpec((kq, n), lambda i: (0, 0)),
            pl.BlockSpec((tm, 1), lambda i: (i, 0)),
            pl.BlockSpec((1, n), lambda i: (0, 0)),
            pl.BlockSpec((tm, 1), lambda i: (i, 0)),
            pl.BlockSpec((1, n), lambda i: (0, 0)),
        ],
        out_specs=pl.BlockSpec((tm, 1), lambda i: (i, 0)),
        out_shape=jax.ShapeDtypeStruct((nr, 1), jnp.float32),
        interpret=INTERPRET,
    )(qa, yat, rb[:, None], cb[None, :], ra[:, None], ca[None, :])[:, 0]


def _col_lse_kernel(qa_ref, yat_ref, rb_ref, cb_ref, ra_ref, ca_ref, out_ref, *, tm):
    tn = yat_ref.shape[1]
    nr = qa_ref.shape[0]
    yat = yat_ref[...]
    cb = cb_ref[...]
    ca = ca_ref[...]

    def body(k, carry):
        m, l = carry
        i = pl.multiple_of(k * tm, tm)
        s = jnp.dot(qa_ref[pl.ds(i, tm), :], yat, preferred_element_type=jnp.float32)
        z = s + ra_ref[pl.ds(i, tm), :] + ca + jnp.maximum(cb - rb_ref[pl.ds(i, tm), :], 0.0)
        m_new = jnp.maximum(m, jnp.max(z, axis=0, keepdims=True))
        l = l * jnp.exp(m - m_new) + jnp.sum(jnp.exp(z - m_new), axis=0, keepdims=True)
        return m_new, l

    m0 = jnp.full((1, tn), -jnp.inf, jnp.float32)
    l0 = jnp.zeros((1, tn), jnp.float32)
    m, l = lax.fori_loop(0, nr // tm, body, (m0, l0))
    out_ref[...] = m + jnp.log(l)


def col_lse(qa, yat, rb, cb, ra, ca, tm=128, tn=512):
    nr, kq = qa.shape
    n = yat.shape[1]
    return pl.pallas_call(
        functools.partial(_col_lse_kernel, tm=tm),
        grid=(n // tn,),
        in_specs=[
            pl.BlockSpec((nr, kq), lambda j: (0, 0)),
            pl.BlockSpec((kq, tn), lambda j: (0, j)),
            pl.BlockSpec((nr, 1), lambda j: (0, 0)),
            pl.BlockSpec((1, tn), lambda j: (0, j)),
            pl.BlockSpec((nr, 1), lambda j: (0, 0)),
            pl.BlockSpec((1, tn), lambda j: (0, j)),
        ],
        out_specs=pl.BlockSpec((1, tn), lambda j: (0, j)),
        out_shape=jax.ShapeDtypeStruct((1, n), jnp.float32),
        interpret=INTERPRET,
    )(qa, yat, rb[:, None], cb[None, :], ra[:, None], ca[None, :])[0]


def _moment_kernel(qa_ref, yat_ref, rb_ref, cb_ref, ra_ref, ca_ref, f_ref, out_ref, *, tn):
    tm = qa_ref.shape[0]
    n = yat_ref.shape[1]
    qa = qa_ref[...]
    rb = rb_ref[...]
    ra = ra_ref[...]

    def body(k, acc):
        j = pl.multiple_of(k * tn, tn)
        s = jnp.dot(qa, yat_ref[:, pl.ds(j, tn)], preferred_element_type=jnp.float32)
        z = s + ra + ca_ref[:, pl.ds(j, tn)] + jnp.maximum(cb_ref[:, pl.ds(j, tn)] - rb, 0.0)
        plan = jnp.exp(z).astype(jnp.bfloat16)
        return acc + jnp.dot(plan, f_ref[pl.ds(j, tn), :], preferred_element_type=jnp.float32)

    acc = lax.fori_loop(0, n // tn, body, jnp.zeros((tm, f_ref.shape[1]), jnp.float32))
    out_ref[...] = acc


def moments(qa, yat, rb, cb, ra, ca, feats, tm=128, tn=512):
    nr, kq = qa.shape
    n = yat.shape[1]
    nf = feats.shape[1]
    return pl.pallas_call(
        functools.partial(_moment_kernel, tn=tn),
        grid=(nr // tm,),
        in_specs=[
            pl.BlockSpec((tm, kq), lambda i: (i, 0)),
            pl.BlockSpec((kq, n), lambda i: (0, 0)),
            pl.BlockSpec((tm, 1), lambda i: (i, 0)),
            pl.BlockSpec((1, n), lambda i: (0, 0)),
            pl.BlockSpec((tm, 1), lambda i: (i, 0)),
            pl.BlockSpec((1, n), lambda i: (0, 0)),
            pl.BlockSpec((n, nf), lambda i: (0, 0)),
        ],
        out_specs=pl.BlockSpec((tm, nf), lambda i: (i, 0)),
        out_shape=jax.ShapeDtypeStruct((nr, nf), jnp.float32),
        interpret=INTERPRET,
    )(qa, yat, rb[:, None], cb[None, :], ra[:, None], ca[None, :], feats)


def merge_lse(parts):
    top = jnp.max(parts, axis=0)
    return top + jnp.log(jnp.sum(jnp.exp(parts - top[None, :]), axis=0))


def on_device(x_points, y_points, row_mass, col_mass, multipliers, col_potential, basket, damping):
    width = x_points.shape[1]
    share = x_points.shape[0]
    x_pack = jnp.concatenate([x_points, multipliers, row_mass[:, None]], axis=1)
    x_rows_pack = gather_col(x_pack)
    x_rows = x_rows_pack[:, :width]
    mult_rows = x_rows_pack[:, width : 2 * width]
    mass_rows = x_rows_pack[:, 2 * width]
    ny = y_points.shape[0]
    own_rmass = jnp.zeros((ny,), jnp.bfloat16).at[:share].set(row_mass)
    y_pack = jnp.concatenate(
        [y_points, col_potential[:, None], col_mass[:, None], own_rmass[:, None]], axis=1
    )
    y_cols_pack = gather_row(y_pack)
    y_cols = y_cols_pack[:, :width]
    pot_cols = y_cols_pack[:, width].astype(jnp.float32)
    mass_cols = y_cols_pack[:, width + 1].astype(jnp.float32)
    rmass_part = jnp.sum(y_cols_pack[:, width + 2].astype(jnp.float32))

    xf = x_rows.astype(jnp.float32)
    hf = mult_rows.astype(jnp.float32)
    yf = y_cols.astype(jnp.float32)
    row_term2 = 2.0 * (-jnp.sum(hf * xf, axis=1) - KAPPA / width * jnp.sum(xf * xf, axis=1))
    row_basket2 = 2.0 * jnp.sum(xf * basket[None, :], axis=1)
    col_term2 = 2.0 * (-(KAPPA / width) * jnp.sum(yf * yf, axis=1))
    col_basket2 = 2.0 * jnp.sum(yf * basket[None, :], axis=1)
    q_core = jnp.concatenate([mult_rows * 2, x_rows * (2.0 * KAPPA / width * 2.0)], axis=1)
    y_t = y_cols.T
    y_core_t = jnp.concatenate([y_t, y_t], axis=0)
    ny_cols = y_cols.shape[0]
    features = jnp.concatenate(
        [yf, yf * yf, jnp.ones((ny_cols, 1), jnp.float32),
         jnp.zeros((ny_cols, KF - 2 * width - 1), jnp.float32)], axis=1
    ).astype(jnp.bfloat16)

    row_weight = mass_rows.astype(jnp.float32)
    log_row = jnp.log(row_weight)
    log_col = jnp.log(mass_cols)
    nrows = x_rows.shape[0]

    gshift = col_term2 + pot_cols / EPS + log_col
    row_local = row_lse(q_core, y_core_t, row_basket2, col_basket2, row_term2, gshift)
    nu_part = jnp.sum(mass_cols)
    row_msg = jnp.concatenate([row_local, jnp.stack([nu_part, rmass_part])])
    row_all = gather_col(row_msg[None, :])
    nu_total = jnp.sum(row_all[:, nrows])
    mu_total = jnp.sum(row_all[:, nrows + 1])
    log_nu_total = jnp.log(nu_total)
    row_potential = -EPS * (merge_lse(row_all[:, :nrows]) - log_nu_total)
    fshift = row_term2 + row_potential / EPS + log_row

    col_local = col_lse(q_core, y_core_t, row_basket2, col_basket2, fshift, col_term2)
    col_all = gather_row(col_local[None, :])
    col_potential_new = -EPS * (merge_lse(col_all) - jnp.log(mu_total))
    gq = col_term2 + col_potential_new / EPS + log_col - log_nu_total
    fq = row_term2 + row_potential / EPS

    both = moments(q_core, y_core_t, row_basket2, col_basket2, fq, gq, features)
    both = both[:, : 2 * width + 1]
    own = lax.psum_scatter(both, COL, scatter_dimension=0, tiled=True)
    first = own[:, :width]
    second = own[:, width : 2 * width]
    own_mass = own[:, 2 * width]
    xo = x_points.astype(jnp.float32)
    grad = first - xo * own_mass[:, None]
    curv = (second - 2.0 * xo * first + xo * xo * own_mass[:, None]) / EPS + RIDGE
    multipliers_new = multipliers.astype(jnp.float32) - damping[None, :] * grad / curv
    return (row_potential, col_potential_new, multipliers_new)


def solution(mesh):
    nrow, ncol = mesh.devices.shape
    split = Mesh(mesh.devices.reshape(nrow // 4, 4, ncol // 2, 2), ROW + COL)
    placed = (
        P(ROW + COL, None),
        P(COL + ROW, None),
        P(ROW + COL),
        P(COL + ROW),
        P(ROW + COL, None),
        P(COL + ROW),
        P(),
        P(),
    )
    return jax.shard_map(
        on_device,
        mesh=split,
        in_specs=placed,
        out_specs=(P(ROW), P(COL), P(ROW + COL, None)),
        check_vma=False,
    )
```

time: 435 us -> 343 us (0.79)
  Pallas kernels: 0 us -> 130 us
  waiting for transfers between devices: 164 us -> 84.8 us
  matrix products: 77.7 us -> 0 us
  loops' own time: 46.6 us -> 0 us
  local copies, waits for them, and re-layouts: 59.4 us -> 21.9 us
  blocking collectives: 37.7 us -> 62.9 us
  other arithmetic: 30.7 us -> 26 us
    pallas_call x0 -> x3, Pallas kernels: none -> 130 us  [the longest x1 48.9 us: row_lse(): pl.pallas_call(functools.partial(_row_lse_kernel, tn=tn), grid=(nr // tm,...]
    all_gather x2, waiting for transfers between devices: 131 us -> 51.5 us  [gather_row(): return lax.all_gather(inner, ROW[0], axis=0, tiled=True)]
    dot_general x32 -> x0, matrix products: 77.7 us -> none  [the longest x24 69.9 us: block_z(): jnp.dot(cut(q_aug, start), y_aug.T, preferred_element_type=jnp.float32)]
    another operation x3 -> x0, loops' own time: 46.6 us -> none  [the longest x1 15.8 us: on_device(): col_tops, col_totals = lax.map(col_pass, starts)]
    dynamic_update_slice x40 -> x0, local copies, waits for them, and re-layouts: 29.8 us -> none  [the longest x16 27.1 us: on_device(): both = lax.map(moment_pass, starts).reshape(nrows, 2 * width + 1)]
    all_gather x1 -> x3, blocking collectives: 13.6 us -> 39 us  [the longest x2 25.3 us: gather_row(): inner = lax.all_gather(value, ROW[1], axis=0, tiled=True)]
    dynamic_slice x72 -> x0, local copies, waits for them, and re-layouts: 17.7 us -> none  [the longest x24 14.1 us: on_device(): row_local = lax.map(row_pass, starts).reshape(nrows)]
    reduce_sum x19 -> x2, other arithmetic: 16.4 us -> 3.59 us  [the longest x1 2.37 us: on_device(): col_term2 = 2.0 * (-(KAPPA / width) * jnp.sum(yf * yf, axis=1))]
  transfers between devices with their start and end apart: 3 -> 3, of which waited for: 3 -> 3; matrix products, arithmetic and copies ran while one was open for 1% -> 4% of each run, Pallas kernels for 0% -> 0%
where the time goes in v2:
time: 343 us; the launch traced here: 342 us
  Pallas kernels  130 us (38%)
  waiting for transfers between devices  84.8 us (25%)
  blocking collectives  62.9 us (18%)
  other arithmetic  26 us (8%)
  local copies, waits for them, and re-layouts  21.9 us (6%)
  between operations  15.9 us (5%)
    all_gather x2, waiting for transfers between devices, gather_row(): return lax.all_gather(inner, ROW[0], axis=0, tiled=True)  51.5 us
    pallas_call x1, Pallas kernels, row_lse(): pl.pallas_call(functools.partial(_row_lse_kernel, tn=tn), grid=(nr // tm,...  48.9 us
    pallas_call x1, Pallas kernels, moments(): pl.pallas_call(functools.partial(_moment_kernel, tn=tn), grid=(nr // tm,)...  46.4 us
    pallas_call x1, Pallas kernels, col_lse(): pl.pallas_call(functools.partial(_col_lse_kernel, tm=tm), grid=(n // tn,)...  34.8 us
    reduce_scatter x1, waiting for transfers between devices, on_device(): own = lax.psum_scatter(both, COL, scatter_dimension=0, tiled=True)  33.3 us
    all_gather x2, blocking collectives, gather_row(): inner = lax.all_gather(value, ROW[1], axis=0, tiled=True)  25.3 us
    unnamed x1, blocking collectives  23.9 us
    all_gather x1, blocking collectives, gather_col(): return lax.all_gather(value, COL, axis=0, tiled=True)  13.6 us
  transfers between devices with their start and end apart: 3, of which 3 were waited for; matrix products, arithmetic and copies ran while one was open for 4% of the time, Pallas kernels for 0%

profile of v2, /device:TPU:2, one launch (start us, length us, event | category | flops | bytes accessed | tf_op | source)
XLA Modules:
  0.0 341.9 jit_solution(14936636318241254286)
XLA Ops:
  7.2 0.8 copy.107
  9.5 0.9 copy.109
  10.5 13.3 %all_gather.19 = bf16[1024,67]{1,0:T(8,128)(2,1)} all-gather(bf16[256,67]{1,0:T(8,128)(2,1)S(1)} %fusion.18), channel_id=1, replica_groups=mesh['z'=8,'x'=4,'y'=4,'core'=2] {'x'}, dimensions={0}, use_global_device_ids=true | all-gather | bytes 171520 | tf_op jit(solution)/shard_map/all_gather | solution.py:19
  23.9 0.8 copy.106
  24.7 0.8 copy.105
  25.7 13.6 %all_gather.18 = bf16[1024,129]{1,0:T(8,128)(2,1)S(1)} all-gather(bf16[128,129]{1,0:T(8,128)(2,1)S(1)} %pad_maximum_fusion.2), channel_id=1, replica_groups=mesh['z'=8,'x'=4,'y'=4,'core'=2] {'y','core'}, dimensions={0}, use_global_device_ids=true | all-gather | bytes 297216 | tf_op jit(solution)/shard_map/all_gather | solution.py:24
  39.3 1.2 fusion.5
  40.5 1.0 copy.113.rb_ref
  41.6 1.1 copy.114.ra_ref
  42.7 1.3 dynamic-slice.7
  44.8 0.9 pad_maximum_fusion.1.qa_ref
  45.7 21.9 %all-gather.6.cloned.1.call-done = bf16[8192,67]{1,0:T(8,128)(2,1)} async-done(((bf16[1024,67]{1,0:T(8,128)(2,1)}), bf16[8192,67]{1,0:T(8,128)(2,1)}) %all-gather.6.cloned.1.call-update) | async-done | bytes 1097744 | tf_op jit(solution)/shard_map/all_gather | solution.py:20
  67.6 3.5 %fusion.19 = (bf16[8192,64]{1,0:T(8,128)(2,1)}, bf16[64,8192]{0,1:T(8,128)(2,1)S(1)}) fusion(bf16[8192,67]{1,0:T(8,128)(2,1)} %all-gather.6.cloned.1.call-done), kind=kLoop, calls=%fused_computation.58 | loop fusion | bytes 3145728 | tf_op jit(solution)/shard_map/slice | solution.py:174
  71.1 2.5 pad_maximum_fusion
  73.6 4.1 %copy.112.yat_ref = bf16[128,8192]{1,0:T(8,128)(2,1)} copy(bf16[128,8192]{0,1:T(8,128)(2,1)} %pad_maximum_fusion) | data formatting | bytes 4194304 | tf_op jit(solution)/shard_map/concatenate | solution.py:188
  77.7 2.4 fusion.1
  80.7 5.1 %convert_reduce_fusion.1 = (f32[]{:T(128)}, f32[]{:T(128)}, f32[8192]{0:T(1024)S(1)}, f32[8192]{0:T(1024)S(1)}) fusion(bf16[8192,67]{1,0:T(8,128)(2,1)S(1)} %copy-done), kind=kLoop, calls=%fused_computation.9 | loop fusion | flops 49150 | bytes 114696 | tf_op jit(solution)/shard_map/reduce_sum | solution.py:177
  86.4 48.9 %shard_map.103 = f32[1024,1]{1,0:T(8,128)} custom-call(bf16[1024,128]{1,0:T(8,128)(2,1)} %pad_maximum_fusion.1.qa_ref, bf16[128,8192]{1,0:T(8,128)(2,1)} %copy.112.yat_ref, f32[1024,1]{1,0:T(8,128)} %copy.113.rb_ref, f32[1,8192]{1,0:T(1,128)} %bitcast.19, f32[1024,1]{1,0:T(8,128)} %copy.114.ra_ref, f32[1,8192]{1,0:T(1,128)} %add_add_fusion.ca_ref), custom_call_target="tpu_custom_call" | custom-call | tf_op jit(solution)/shard_map/pallas_call | solution.py:56
  135.3 1.4 reduce.9
  136.7 1.4 concatenate.25
  138.4 23.9 %all-reduce.1 = f32[8208]{0:T(1024)S(1)} all-reduce(f32[8208]{0:T(1024)S(1)} %dynamic-update-slice.3), channel_id=2, replica_groups=mesh['z'=8,'x'=4,'y'=4,'core'=2] {'y','core'}, use_global_device_ids=true, to_apply=%add.1 | all-reduce | flops 8208 | bytes 65664
  165.4 1.0 log_add_fusion.ra_ref
  166.4 34.8 %shard_map.104 = f32[1,8192]{1,0:T(1,128)} custom-call(bf16[1024,128]{1,0:T(8,128)(2,1)} %pad_maximum_fusion.1.qa_ref, bf16[128,8192]{1,0:T(8,128)(2,1)} %copy.112.yat_ref, f32[1024,1]{1,0:T(8,128)} %copy.113.rb_ref, f32[1,8192]{1,0:T(1,128)} %bitcast.20, f32[1024,1]{1,0:T(8,128)} %log_add_fusion.ra_ref, f32[1,8192]{1,0:T(1,128)} %bitcast.23), custom_call_target="tpu_custom_call" | custom-call | tf_op jit(solution)/shard_map/pallas_call | solution.py:98
  201.2 12.0 %all-gather.1 = f32[4,1,8192]{2,1,0:T(1,128)S(1)} all-gather(f32[1,1,8192]{2,1,0:T(1,128)} %bitcast.28), channel_id=1, replica_groups=mesh['z'=8,'x'=4,'y'=4,'core'=2] {'x'}, dimensions={0}, use_global_device_ids=true | all-gather | bytes 163840 | tf_op jit(solution)/shard_map/all_gather | solution.py:19
  214.2 4.7 %maximum_maximum_fusion.f_ref = bf16[8192,256]{1,0:T(8,128)(2,1)} fusion(bf16[8192,64]{1,0:T(8,128)(2,1)} %get-tuple-element.46, bf16[8192,64]{1,0:T(8,128)(2,1)S(1)} %copy-done.1, bf16[256]{0:T(256)(128)(2,1)S(1)} %pad.6.clone, bf16[256]{0:T(256)(128)(2,1)S(1)} %pad.5.clone), kind=kLoop, calls=%fused_computation.8 | loop fusion | flops 16777216 | bytes 6292480 | tf_op jit(solution)/shard_map/concatenate | solution.py:190
  218.9 29.5 %all-gather.8.cloned.1.call-done = f32[8,4,8192]{2,1,0:T(4,128)} async-done(((f32[1,4,8192]{2,1,0:T(4,128)}), f32[8,4,8192]{2,1,0:T(4,128)}) %all-gather.8.cloned.1.call-update) | async-done | bytes 1048592 | tf_op jit(solution)/shard_map/all_gather | solution.py:20
  248.5 1.6 reshape.222
  250.0 1.4 reduce_max.19
  253.0 46.4 %shard_map.105 = f32[1024,256]{1,0:T(8,128)} custom-call(bf16[1024,128]{1,0:T(8,128)(2,1)} %pad_maximum_fusion.1.qa_ref, bf16[128,8192]{1,0:T(8,128)(2,1)} %copy.112.yat_ref, f32[1024,1]{1,0:T(8,128)} %copy.113.rb_ref, f32[1,8192]{1,0:T(1,128)} %bitcast.21, f32[1024,1]{1,0:T(8,128)} %copy-done.2, f32[1,8192]{1,0:T(1,128)} %add_subtract_fusion.ca_ref, ...), custom_call_target="tpu_custom_call" | custom-call | tf_op jit(solution)/shard_map/pallas_call | solution.py:137
  299.4 33.3 %reduce-scatter.2.cloned.1.call-done = f32[128,129]{1,0:T(8,128)} async-done(((f32[1024,129]{1,0:T(8,128)}), f32[128,129]{1,0:T(8,128)}) %reduce-scatter.2.cloned.1.call-update) | async-done | bytes 66064 | tf_op jit(solution)/shard_map/reduce_scatter | solution.py:219
  332.7 0.9 slice_reduce_fusion
  333.7 1.0 fusion.11
  (45 shorter events, 8.4 us)
Async XLA Ops:
  7.2 60.4 %all-gather.6.cloned.1.call-start = ((), (), s32[]{:S(2)}) async-start(), calls=%async_computation.1 | async-start | bytes 2359296 | tf_op jit(solution)/shard_map/all_gather | solution.py:20
  23.8 224.6 %all-gather.8.cloned.1.call-start = ((), (), s32[]{:S(2)}) async-start(), calls=%async_computation.3 | async-start | bytes 1179648 | tf_op jit(solution)/shard_map/all_gather | solution.py:20
  71.1 6.6 %copy-start = (bf16[8192,67]{1,0:T(8,128)(2,1)S(1)}, bf16[8192,67]{1,0:T(8,128)(2,1)}, u32[]{:S(2)}) copy-start(bf16[8192,67]{1,0:T(8,128)(2,1)} %all-gather.6.cloned.1.call-done) | copy-start | bytes 3293188
  71.1 6.6 %copy-start.5 = (f32[64]{0:T(128)S(1)}, f32[64]{0:T(128)}, u32[]{:S(2)}) copy-start(f32[64]{0:T(128)} %param.16) | copy-start | bytes 772
  80.7 54.6 %copy-start.3 = (f32[8192]{0:T(1024)}, f32[8192]{0:T(1024)S(1)}, u32[]{:S(2)}) copy-start(f32[8192]{0:T(1024)S(1)} %get-tuple-element.55) | copy-start | bytes 98308
  135.3 78.9 %copy-start.1 = (bf16[8192,64]{1,0:T(8,128)(2,1)S(1)}, bf16[8192,64]{1,0:T(8,128)(2,1)}, u32[]{:S(2)}) copy-start(bf16[8192,64]{1,0:T(8,128)(2,1)} %get-tuple-element.44) | copy-start | bytes 3145732
  165.4 53.6 %copy-start.2 = (f32[1024,1]{1,0:T(8,128)}, f32[1024,1]{1,0:T(8,128)S(1)}, u32[]{:S(2)}) copy-start(f32[1024,1]{1,0:T(8,128)S(1)} %copy.116.ra_ref) | copy-start | bytes 12292
  214.0 118.7 %reduce-scatter.2.cloned.1.call-start = ((), (), s32[]{:S(2)}) async-start(), calls=%async_computation.2 | async-start | bytes 1179648 | tf_op jit(solution)/shard_map/reduce_scatter | solution.py:219
  218.9 33.4 %copy-start.4 = (f32[8192]{0:T(1024)S(1)}, f32[8192]{0:T(1024)}, u32[]{:S(2)}) copy-start(f32[8192]{0:T(1024)} %copy-done.3) | copy-start | bytes 98308
  253.0 80.7 %copy-start.6 = (f32[64]{0:T(128)S(1)}, f32[64]{0:T(128)}, u32[]{:S(2)}) copy-start(f32[64]{0:T(128)} %param.17) | copy-start | bytes 772
Sparse Core Ops, SparseCore 0:
  24.0 43.5 all-gather.5
  214.1 34.2 all-gather.7
  299.5 33.1 reduce-scatter.1

commit v3 on v2

--- a/solution.py
+++ b/solution.py
@@ -18,6 +18,13 @@
 def gather_row(value):
     inner = lax.all_gather(value, ROW[1], axis=0, tiled=True)
     return lax.all_gather(inner, ROW[0], axis=0, tiled=True)
+
+
+def gather_row_z_first(value):
+    inner = lax.all_gather(value, ROW[0], axis=0)
+    outer = lax.all_gather(inner, ROW[1], axis=0)
+    outer = jnp.swapaxes(outer, 0, 1)
+    return outer.reshape((-1,) + value.shape[1:])
 
 
 def gather_col(value):
@@ -95,6 +102,7 @@
 def col_lse(qa, yat, rb, cb, ra, ca, tm=128, tn=512):
     nr, kq = qa.shape
     n = yat.shape[1]
+    tn = min(tn, n)
     return pl.pallas_call(
         functools.partial(_col_lse_kernel, tm=tm),
         grid=(n // tn,),
@@ -170,7 +178,7 @@
     y_pack = jnp.concatenate(
         [y_points, col_potential[:, None], col_mass[:, None], own_rmass[:, None]], axis=1
     )
-    y_cols_pack = gather_row(y_pack)
+    y_cols_pack = gather_row_z_first(y_pack)
     y_cols = y_cols_pack[:, :width]
     pot_cols = y_cols_pack[:, width].astype(jnp.float32)
     mass_cols = y_cols_pack[:, width + 1].astype(jnp.float32)
@@ -198,7 +206,8 @@
     nrows = x_rows.shape[0]
 
     gshift = col_term2 + pot_cols / EPS + log_col
-    row_local = row_lse(q_core, y_core_t, row_basket2, col_basket2, row_term2, gshift)
+    y_core = jnp.concatenate([y_cols, y_cols], axis=1)
+    row_local = col_lse(y_core, q_core.T, -col_basket2, -row_basket2, gshift, row_term2)
     nu_part = jnp.sum(mass_cols)
     row_msg = jnp.concatenate([row_local, jnp.stack([nu_part, rmass_part])])
     row_all = gather_col(row_msg[None, :])

time: 343 us -> 344 us (level)
  blocking collectives: 62.9 us -> 78.8 us
  waiting for transfers between devices: 84.8 us -> 70.3 us
  Pallas kernels: 130 us -> 118 us
  local copies, waits for them, and re-layouts: 21.9 us -> 28.5 us
  other arithmetic: 26 us -> 31.9 us
    pallas_call x1 -> x0, Pallas kernels: 48.9 us -> none  [row_lse(): pl.pallas_call(functools.partial(_row_lse_kernel, tn=tn), grid=(nr // tm,...]
    pallas_call x1 -> x2, Pallas kernels: 34.8 us -> 71.7 us  [col_lse(): pl.pallas_call(functools.partial(_col_lse_kernel, tm=tm), grid=(n // tn,)...]
    all_gather x0 -> x1, blocking collectives: none -> 28.6 us  [gather_row_z_first(): inner = lax.all_gather(value, ROW[0], axis=0)]
    all_gather x2 -> x1, waiting for transfers between devices: 51.5 us -> 31.8 us  [gather_row(): return lax.all_gather(inner, ROW[0], axis=0, tiled=True)]
    all_gather x2 -> x1, blocking collectives: 25.3 us -> 11.9 us  [gather_row(): inner = lax.all_gather(value, ROW[1], axis=0, tiled=True)]
    log x0 -> x1, other arithmetic: none -> 7.48 us  [on_device(): log_col = jnp.log(mass_cols)]
    transpose x0 -> x3, local copies, waits for them, and re-layouts: none -> 6.22 us  [the longest x1 3.08 us: gather_row_z_first(): outer = jnp.swapaxes(outer, 0, 1)]
    all_gather x0 -> x1, waiting for transfers between devices: none -> 5.14 us  [gather_row_z_first(): outer = lax.all_gather(inner, ROW[1], axis=0)]
where the time goes in v3:
time: 344 us
  Pallas kernels  118 us (34%)
  blocking collectives  78.8 us (23%)
  waiting for transfers between devices  70.3 us (20%)
  other arithmetic  31.9 us (9%)
  local copies, waits for them, and re-layouts  28.5 us (8%)
  between operations  15.9 us (5%)
    pallas_call x2, Pallas kernels, col_lse(): pl.pallas_call(functools.partial(_col_lse_kernel, tm=tm), grid=(n // tn,)...  71.7 us
    pallas_call x1, Pallas kernels, moments(): pl.pallas_call(functools.partial(_moment_kernel, tn=tn), grid=(nr // tm,)...  46.4 us
    reduce_scatter x1, waiting for transfers between devices, on_device(): own = lax.psum_scatter(both, COL, scatter_dimension=0, tiled=True)  33.3 us
    all_gather x1, waiting for transfers between devices, gather_row(): return lax.all_gather(inner, ROW[0], axis=0, tiled=True)  31.8 us
    all_gather x1, blocking collectives, gather_row_z_first(): inner = lax.all_gather(value, ROW[0], axis=0)  28.6 us
    unnamed x1, blocking collectives  24.6 us
    all_gather x1, blocking collectives, gather_col(): return lax.all_gather(value, COL, axis=0, tiled=True)  13.6 us
    all_gather x1, blocking collectives, gather_row(): inner = lax.all_gather(value, ROW[1], axis=0, tiled=True)  11.9 us
  transfers between devices with their start and end apart: 3, of which 3 were waited for; matrix products, arithmetic and copies ran while one was open for 4% of the time, Pallas kernels for 0%

profile of v3, /device:TPU:2, one launch (start us, length us, event | category | flops | bytes accessed | tf_op | source)
XLA Modules:
  0.0 343.6 jit_solution(5612937275650281357)
XLA Ops:
  9.3 28.6 %all-gather = bf16[2048,67]{0,1:T(8,128)(2,1)S(1)} all-gather(bf16[256,67]{0,1:T(8,128)(2,1)S(1)} %fusion.19), channel_id=2, replica_groups=mesh['z'=8,'x'=4,'y'=4,'core'=2] {'z'}, dimensions={0}, use_global_device_ids=true | all-gather | bytes 308736 | tf_op jit(solution)/shard_map/all_gather | solution.py:24
  38.8 0.8 copy.94
  39.6 0.8 copy.92
  40.4 0.8 copy.93
  41.4 13.6 %all_gather.28 = bf16[1024,129]{1,0:T(8,128)(2,1)S(1)} all-gather(bf16[128,129]{1,0:T(8,128)(2,1)S(1)} %pad_maximum_fusion.3), channel_id=1, replica_groups=mesh['z'=8,'x'=4,'y'=4,'core'=2] {'y','core'}, dimensions={0}, use_global_device_ids=true | all-gather | bytes 297216 | tf_op jit(solution)/shard_map/all_gather | solution.py:31
  55.3 0.8 copy.96.yat_ref
  57.3 1.0 copy.101.rb_ref
  59.7 0.9 pad_maximum_fusion.2.qa_ref
  60.6 5.1 %all-gather.8.cloned.1.call-done = bf16[32,256,67]{1,0,2:T(8,128)(2,1)} async-done(((bf16[8,256,67]{1,0,2:T(8,128)(2,1)}), bf16[32,256,67]{1,0,2:T(8,128)(2,1)}) %all-gather.8.cloned.1.call-update) | async-done | bytes 1097744 | tf_op jit(solution)/shard_map/all_gather | solution.py:25
  65.7 3.1 copy.91
  68.8 2.4 fusion.1
  71.2 2.3 slice_bitcast_fusion.1
  73.5 2.7 copy.95
  76.2 7.5 %fusion.2 = (f32[8192]{0:T(1024)S(1)}, f32[]{:T(128)}, f32[]{:T(128)}, f32[8192,1]{1,0:T(8,128)}) fusion(bf16[8192,67]{1,0:T(8,128)(2,1)S(1)} %bitcast.35, f32[8192,1]{1,0:T(8,128)} %copy.95), kind=kLoop, calls=%fused_computation.6 | loop fusion | flops 65534 | bytes 147464 | tf_op jit(solution)/shard_map/log | solution.py:205
  84.3 2.6 copy.97.rb_ref
  86.9 2.5 pad_maximum_fusion.qa_ref
  89.4 36.9 %shard_map.103 = f32[1,1024]{1,0:T(1,128)} custom-call(bf16[8192,128]{1,0:T(8,128)(2,1)} %pad_maximum_fusion.qa_ref, bf16[128,1024]{1,0:T(8,128)(2,1)} %copy.96.yat_ref, f32[8192,1]{1,0:T(8,128)} %copy.97.rb_ref, f32[1,1024]{1,0:T(1,128)} %bitcast.52, f32[8192,1]{1,0:T(8,128)} %get-tuple-element.46.ra_ref, f32[1,1024]{1,0:T(1,128)} %bitcast.50), custom_call_target="tpu_custom_call" | custom-call | tf_op jit(solution)/shard_map/pallas_call | solution.py:106
  126.3 2.1 concatenate.28
  128.7 24.6 %all-reduce.1 = f32[8208]{0:T(1024)S(1)} all-reduce(f32[8208]{0:T(1024)S(1)} %dynamic-update-slice.3), channel_id=4, replica_groups=mesh['z'=8,'x'=4,'y'=4,'core'=2] {'y','core'}, use_global_device_ids=true, to_apply=%add.1 | all-reduce | flops 8208 | bytes 65664
  155.6 1.0 log_add_fusion.ra_ref
  156.7 4.7 %pad_maximum_fusion.1 = bf16[128,8192]{0,1:T(8,128)(2,1)} fusion(bf16[64,8192]{0,1:T(8,128)(2,1)} %get-tuple-element.44), kind=kLoop, calls=%fused_computation.12 | loop fusion | flops 4194304 | bytes 3145728 | tf_op jit(solution)/shard_map/concatenate | solution.py:196
  161.4 4.1 %copy.100.yat_ref = bf16[128,8192]{1,0:T(8,128)(2,1)} copy(bf16[128,8192]{0,1:T(8,128)(2,1)} %pad_maximum_fusion.1) | data formatting | bytes 4194304 | tf_op jit(solution)/shard_map/concatenate | solution.py:196
  165.5 34.8 %shard_map.104 = f32[1,8192]{1,0:T(1,128)} custom-call(bf16[1024,128]{1,0:T(8,128)(2,1)} %pad_maximum_fusion.2.qa_ref, bf16[128,8192]{1,0:T(8,128)(2,1)} %copy.100.yat_ref, f32[1024,1]{1,0:T(8,128)} %copy.101.rb_ref, f32[1,8192]{1,0:T(1,128)} %bitcast.44, f32[1024,1]{1,0:T(8,128)} %log_add_fusion.ra_ref, f32[1,8192]{1,0:T(1,128)} %bitcast.41), custom_call_target="tpu_custom_call" | custom-call | tf_op jit(solution)/shard_map/pallas_call | solution.py:106
  200.4 11.9 %all-gather.3 = f32[4,1,8192]{2,1,0:T(1,128)S(1)} all-gather(f32[1,1,8192]{2,1,0:T(1,128)} %bitcast.47), channel_id=1, replica_groups=mesh['z'=8,'x'=4,'y'=4,'core'=2] {'x'}, dimensions={0}, use_global_device_ids=true | all-gather | bytes 163840 | tf_op jit(solution)/shard_map/all_gather | solution.py:19
  213.7 4.7 %maximum_maximum_fusion.f_ref = bf16[8192,256]{1,0:T(8,128)(2,1)} fusion(bf16[8192,64]{1,0:T(8,128)(2,1)} %get-tuple-element.43, bf16[8192,64]{1,0:T(8,128)(2,1)S(1)} %copy-done, bf16[256]{0:T(256)(128)(2,1)S(1)} %pad.6.clone, bf16[256]{0:T(256)(128)(2,1)S(1)} %pad.5.clone), kind=kLoop, calls=%fused_computation.9 | loop fusion | flops 16777216 | bytes 6292480 | tf_op jit(solution)/shard_map/concatenate | solution.py:198
  218.4 31.8 %all-gather.10.cloned.1.call-done = f32[8,4,8192]{2,1,0:T(4,128)} async-done(((f32[1,4,8192]{2,1,0:T(4,128)}), f32[8,4,8192]{2,1,0:T(4,128)}) %all-gather.10.cloned.1.call-update) | async-done | bytes 1048592 | tf_op jit(solution)/shard_map/all_gather | solution.py:20
  250.1 1.6 reshape.252
  251.7 1.4 reduce_max.19
  254.6 46.4 %shard_map.105 = f32[1024,256]{1,0:T(8,128)} custom-call(bf16[1024,128]{1,0:T(8,128)(2,1)} %pad_maximum_fusion.2.qa_ref, bf16[128,8192]{1,0:T(8,128)(2,1)} %copy.100.yat_ref, f32[1024,1]{1,0:T(8,128)} %copy.101.rb_ref, f32[1,8192]{1,0:T(1,128)} %bitcast.45, f32[1024,1]{1,0:T(8,128)} %copy-done.1, f32[1,8192]{1,0:T(1,128)} %add_subtract_fusion.ca_ref, ...), custom_call_target="tpu_custom_call" | custom-call | tf_op jit(solution)/shard_map/pallas_call | solution.py:145
  301.1 33.3 %reduce-scatter.2.cloned.1.call-done = f32[128,129]{1,0:T(8,128)} async-done(((f32[1024,129]{1,0:T(8,128)}), f32[128,129]{1,0:T(8,128)}) %reduce-scatter.2.cloned.1.call-update) | async-done | bytes 66064 | tf_op jit(solution)/shard_map/reduce_scatter | solution.py:228
  334.4 0.9 slice_reduce_fusion
  335.3 1.0 fusion.12
  (51 shorter events, 10.7 us)
Async XLA Ops:
  7.2 51.3 %copy-start.7 = (u32[256]{0:T(256)S(1)}, u32[256]{0:T(256)}, u32[]{:S(2)}) copy-start(u32[256]{0:T(256)} %constant.71) | copy-start | bytes 3076
  7.2 49.0 %copy-start.5 = (f32[64]{0:T(128)S(1)}, f32[64]{0:T(128)}, u32[]{:S(2)}) copy-start(f32[64]{0:T(128)} %param.16) | copy-start | bytes 772
  7.2 58.5 %all-gather.8.cloned.1.call-start = ((), (), s32[]{:S(2)}) async-start(), calls=%async_computation.2 | async-start | bytes 1372160 | tf_op jit(solution)/shard_map/all_gather | solution.py:25
  38.8 211.4 %all-gather.10.cloned.1.call-start = ((), (), s32[]{:S(2)}) async-start(), calls=%async_computation.3 | async-start | bytes 1179648 | tf_op jit(solution)/shard_map/all_gather | solution.py:20
  73.5 10.1 %copy-start.2 = (f32[8192]{0:T(1024)}, f32[8192]{0:T(1024)S(1)}, u32[]{:S(2)}) copy-start(f32[8192]{0:T(1024)S(1)} %broadcast_multiply_fusion.2) | copy-start | bytes 98308
  83.7 3.2 copy-start
  89.4 65.4 %copy-start.4 = (f32[1024]{0:T(1024)S(1)}, f32[1024]{0:T(1024)}, u32[]{:S(2)}) copy-start(f32[1024]{0:T(1024)} %get-tuple-element.57) | copy-start | bytes 12292
  155.6 9.9 %copy-start.1 = (f32[1024,1]{1,0:T(8,128)}, f32[1024,1]{1,0:T(8,128)S(1)}, u32[]{:S(2)}) copy-start(f32[1024,1]{1,0:T(8,128)S(1)} %copy.99.ra_ref) | copy-start | bytes 12292
  213.0 121.4 %reduce-scatter.2.cloned.1.call-start = ((), (), s32[]{:S(2)}) async-start(), calls=%async_computation.1 | async-start | bytes 1179648 | tf_op jit(solution)/shard_map/reduce_scatter | solution.py:228
  218.4 35.6 %copy-start.3 = (f32[8192]{0:T(1024)S(1)}, f32[8192]{0:T(1024)}, u32[]{:S(2)}) copy-start(f32[8192]{0:T(1024)} %copy-done.2) | copy-start | bytes 98308
  254.6 80.7 %copy-start.6 = (f32[64]{0:T(128)S(1)}, f32[64]{0:T(128)}, u32[]{:S(2)}) copy-start(f32[64]{0:T(128)} %param.17) | copy-start | bytes 772
Sparse Core Ops, SparseCore 0:
  38.9 26.7 all-gather.7
  213.1 36.9 all-gather.9
  301.2 33.1 reduce-scatter.1

commit v4 on v3

--- a/solution.py
+++ b/solution.py
@@ -99,9 +99,10 @@
     out_ref[...] = m + jnp.log(l)
 
 
-def col_lse(qa, yat, rb, cb, ra, ca, tm=128, tn=512):
+def col_lse(qa, yat, rb, cb, ra, ca, tm=512, tn=1024):
     nr, kq = qa.shape
     n = yat.shape[1]
+    tm = min(tm, nr)
     tn = min(tn, n)
     return pl.pallas_call(
         functools.partial(_col_lse_kernel, tm=tm),
@@ -138,9 +139,11 @@
     out_ref[...] = acc
 
 
-def moments(qa, yat, rb, cb, ra, ca, feats, tm=128, tn=512):
+def moments(qa, yat, rb, cb, ra, ca, feats, tm=512, tn=2048):
     nr, kq = qa.shape
     n = yat.shape[1]
+    tm = min(tm, nr)
+    tn = min(tn, n)
     nf = feats.shape[1]
     return pl.pallas_call(
         functools.partial(_moment_kernel, tn=tn),

time: 344 us -> 280 us (0.81)
  Pallas kernels: 118 us -> 54.1 us
    pallas_call x2, Pallas kernels: 71.7 us -> 37.6 us  [col_lse(): pl.pallas_call(functools.partial(_col_lse_kernel, tm=tm), grid=(n // tn,)...]
    pallas_call x1, Pallas kernels: 46.4 us -> 16.5 us  [moments(): pl.pallas_call(functools.partial(_moment_kernel, tn=tn), grid=(nr // tm,)...]
where the time goes in v4:
time: 280 us
  blocking collectives  78.8 us (28%)
  waiting for transfers between devices  70.3 us (25%)
  Pallas kernels  54.1 us (19%)
  other arithmetic  31.9 us (11%)
  local copies, waits for them, and re-layouts  28.5 us (10%)
  between operations  15.9 us (6%)
    pallas_call x2, Pallas kernels, col_lse(): pl.pallas_call(functools.partial(_col_lse_kernel, tm=tm), grid=(n // tn,)...  37.6 us
    reduce_scatter x1, waiting for transfers between devices, on_device(): own = lax.psum_scatter(both, COL, scatter_dimension=0, tiled=True)  33.3 us
    all_gather x1, waiting for transfers between devices, gather_row(): return lax.all_gather(inner, ROW[0], axis=0, tiled=True)  31.8 us
    all_gather x1, blocking collectives, gather_row_z_first(): inner = lax.all_gather(value, ROW[0], axis=0)  28.6 us
    unnamed x1, blocking collectives  24.6 us
    pallas_call x1, Pallas kernels, moments(): pl.pallas_call(functools.partial(_moment_kernel, tn=tn), grid=(nr // tm,)...  16.5 us
    all_gather x1, blocking collectives, gather_col(): return lax.all_gather(value, COL, axis=0, tiled=True)  13.6 us
    all_gather x1, blocking collectives, gather_row(): inner = lax.all_gather(value, ROW[1], axis=0, tiled=True)  11.9 us
  transfers between devices with their start and end apart: 3, of which 3 were waited for; matrix products, arithmetic and copies ran while one was open for 4% of the time, Pallas kernels for 0%

profile of v4, /device:TPU:2, one launch (start us, length us, event | category | flops | bytes accessed | tf_op | source)
XLA Modules:
  0.0 279.6 jit_solution(3734354820889971858)
XLA Ops:
  9.3 28.6 %all-gather = bf16[2048,67]{0,1:T(8,128)(2,1)S(1)} all-gather(bf16[256,67]{0,1:T(8,128)(2,1)S(1)} %fusion.19), channel_id=2, replica_groups=mesh['z'=8,'x'=4,'y'=4,'core'=2] {'z'}, dimensions={0}, use_global_device_ids=true | all-gather | bytes 308736 | tf_op jit(solution)/shard_map/all_gather | solution.py:24
  38.8 0.8 copy.94
  39.6 0.8 copy.92
  40.4 0.8 copy.93
  41.4 13.6 %all_gather.28 = bf16[1024,129]{1,0:T(8,128)(2,1)S(1)} all-gather(bf16[128,129]{1,0:T(8,128)(2,1)S(1)} %pad_maximum_fusion.3), channel_id=1, replica_groups=mesh['z'=8,'x'=4,'y'=4,'core'=2] {'y','core'}, dimensions={0}, use_global_device_ids=true | all-gather | bytes 297216 | tf_op jit(solution)/shard_map/all_gather | solution.py:31
  55.3 0.8 copy.96.yat_ref
  57.3 1.0 copy.101.rb_ref
  59.7 0.9 pad_maximum_fusion.2.qa_ref
  60.6 5.1 %all-gather.8.cloned.1.call-done = bf16[32,256,67]{1,0,2:T(8,128)(2,1)} async-done(((bf16[8,256,67]{1,0,2:T(8,128)(2,1)}), bf16[32,256,67]{1,0,2:T(8,128)(2,1)}) %all-gather.8.cloned.1.call-update) | async-done | bytes 1097744 | tf_op jit(solution)/shard_map/all_gather | solution.py:25
  65.7 3.1 %copy.91 = bf16[8,4,256,67]{3,2,1,0:T(8,128)(2,1)S(1)} copy(bf16[8,4,256,67]{2,0,1,3:T(8,128)(2,1)} %bitcast.39) | data formatting | bytes 2195456 | tf_op jit(solution)/shard_map/transpose | solution.py:26
  68.8 2.4 fusion.1
  71.2 2.3 slice_bitcast_fusion.1
  73.5 2.7 copy.95
  76.2 7.5 %fusion.2 = (f32[8192]{0:T(1024)S(1)}, f32[]{:T(128)}, f32[]{:T(128)}, f32[8192,1]{1,0:T(8,128)}) fusion(bf16[8192,67]{1,0:T(8,128)(2,1)S(1)} %bitcast.35, f32[8192,1]{1,0:T(8,128)} %copy.95), kind=kLoop, calls=%fused_computation.6 | loop fusion | flops 65534 | bytes 147464 | tf_op jit(solution)/shard_map/log | solution.py:208
  84.3 2.6 copy.97.rb_ref
  86.9 2.5 pad_maximum_fusion.qa_ref
  89.4 20.0 %shard_map.103 = f32[1,1024]{1,0:T(1,128)} custom-call(bf16[8192,128]{1,0:T(8,128)(2,1)} %pad_maximum_fusion.qa_ref, bf16[128,1024]{1,0:T(8,128)(2,1)} %copy.96.yat_ref, f32[8192,1]{1,0:T(8,128)} %copy.97.rb_ref, f32[1,1024]{1,0:T(1,128)} %bitcast.52, f32[8192,1]{1,0:T(8,128)} %get-tuple-element.46.ra_ref, f32[1,1024]{1,0:T(1,128)} %bitcast.50), custom_call_target="tpu_custom_call" | custom-call | tf_op jit(solution)/shard_map/pallas_call | solution.py:107
  109.4 2.1 concatenate.28
  111.7 24.6 %all-reduce.1 = f32[8208]{0:T(1024)S(1)} all-reduce(f32[8208]{0:T(1024)S(1)} %dynamic-update-slice.3), channel_id=4, replica_groups=mesh['z'=8,'x'=4,'y'=4,'core'=2] {'y','core'}, use_global_device_ids=true, to_apply=%add.1 | all-reduce | flops 8208 | bytes 65664
  138.7 1.0 log_add_fusion.ra_ref
  139.8 4.7 %pad_maximum_fusion.1 = bf16[128,8192]{0,1:T(8,128)(2,1)} fusion(bf16[64,8192]{0,1:T(8,128)(2,1)} %get-tuple-element.44), kind=kLoop, calls=%fused_computation.12 | loop fusion | flops 4194304 | bytes 3145728 | tf_op jit(solution)/shard_map/concatenate | solution.py:199
  144.5 4.1 %copy.100.yat_ref = bf16[128,8192]{1,0:T(8,128)(2,1)} copy(bf16[128,8192]{0,1:T(8,128)(2,1)} %pad_maximum_fusion.1) | data formatting | bytes 4194304 | tf_op jit(solution)/shard_map/concatenate | solution.py:199
  148.6 17.6 %shard_map.104 = f32[1,8192]{1,0:T(1,128)} custom-call(bf16[1024,128]{1,0:T(8,128)(2,1)} %pad_maximum_fusion.2.qa_ref, bf16[128,8192]{1,0:T(8,128)(2,1)} %copy.100.yat_ref, f32[1024,1]{1,0:T(8,128)} %copy.101.rb_ref, f32[1,8192]{1,0:T(1,128)} %bitcast.44, f32[1024,1]{1,0:T(8,128)} %log_add_fusion.ra_ref, f32[1,8192]{1,0:T(1,128)} %bitcast.41), custom_call_target="tpu_custom_call" | custom-call | tf_op jit(solution)/shard_map/pallas_call | solution.py:107
  166.2 11.9 %all-gather.3 = f32[4,1,8192]{2,1,0:T(1,128)S(1)} all-gather(f32[1,1,8192]{2,1,0:T(1,128)} %bitcast.47), channel_id=1, replica_groups=mesh['z'=8,'x'=4,'y'=4,'core'=2] {'x'}, dimensions={0}, use_global_device_ids=true | all-gather | bytes 163840 | tf_op jit(solution)/shard_map/all_gather | solution.py:19
  179.5 4.7 %maximum_maximum_fusion.f_ref = bf16[8192,256]{1,0:T(8,128)(2,1)} fusion(bf16[8192,64]{1,0:T(8,128)(2,1)} %get-tuple-element.43, bf16[8192,64]{1,0:T(8,128)(2,1)S(1)} %copy-done, bf16[256]{0:T(256)(128)(2,1)S(1)} %pad.6.clone, bf16[256]{0:T(256)(128)(2,1)S(1)} %pad.5.clone), kind=kLoop, calls=%fused_computation.9 | loop fusion | flops 16777216 | bytes 6292480 | tf_op jit(solution)/shard_map/concatenate | solution.py:201
  184.2 31.8 %all-gather.10.cloned.1.call-done = f32[8,4,8192]{2,1,0:T(4,128)} async-done(((f32[1,4,8192]{2,1,0:T(4,128)}), f32[8,4,8192]{2,1,0:T(4,128)}) %all-gather.10.cloned.1.call-update) | async-done | bytes 1048592 | tf_op jit(solution)/shard_map/all_gather | solution.py:20
  216.0 1.6 reshape.252
  217.6 1.4 reduce_max.19
  220.5 16.5 %shard_map.105 = f32[1024,256]{1,0:T(8,128)} custom-call(bf16[1024,128]{1,0:T(8,128)(2,1)} %pad_maximum_fusion.2.qa_ref, bf16[128,8192]{1,0:T(8,128)(2,1)} %copy.100.yat_ref, f32[1024,1]{1,0:T(8,128)} %copy.101.rb_ref, f32[1,8192]{1,0:T(1,128)} %bitcast.45, f32[1024,1]{1,0:T(8,128)} %copy-done.1, f32[1,8192]{1,0:T(1,128)} %add_subtract_fusion.ca_ref, ...), custom_call_target="tpu_custom_call" | custom-call | tf_op jit(solution)/shard_map/pallas_call | solution.py:148
  237.0 33.3 %reduce-scatter.2.cloned.1.call-done = f32[128,129]{1,0:T(8,128)} async-done(((f32[1024,129]{1,0:T(8,128)}), f32[128,129]{1,0:T(8,128)}) %reduce-scatter.2.cloned.1.call-update) | async-done | bytes 66064 | tf_op jit(solution)/shard_map/reduce_scatter | solution.py:231
  270.4 0.9 slice_reduce_fusion
  271.3 1.0 fusion.12
  (51 shorter events, 10.7 us)
Async XLA Ops:
  7.2 51.3 %copy-start.7 = (u32[256]{0:T(256)S(1)}, u32[256]{0:T(256)}, u32[]{:S(2)}) copy-start(u32[256]{0:T(256)} %constant.71) | copy-start | bytes 3076
  7.2 49.0 %copy-start.5 = (f32[64]{0:T(128)S(1)}, f32[64]{0:T(128)}, u32[]{:S(2)}) copy-start(f32[64]{0:T(128)} %param.16) | copy-start | bytes 772
  7.2 58.5 %all-gather.8.cloned.1.call-start = ((), (), s32[]{:S(2)}) async-start(), calls=%async_computation.2 | async-start | bytes 1372160 | tf_op jit(solution)/shard_map/all_gather | solution.py:25
  38.8 177.2 %all-gather.10.cloned.1.call-start = ((), (), s32[]{:S(2)}) async-start(), calls=%async_computation.3 | async-start | bytes 1179648 | tf_op jit(solution)/shard_map/all_gather | solution.py:20
  73.5 10.1 %copy-start.2 = (f32[8192]{0:T(1024)}, f32[8192]{0:T(1024)S(1)}, u32[]{:S(2)}) copy-start(f32[8192]{0:T(1024)S(1)} %broadcast_multiply_fusion.2) | copy-start | bytes 98308
  83.7 3.2 %copy-start = (bf16[8192,64]{1,0:T(8,128)(2,1)S(1)}, bf16[8192,64]{1,0:T(8,128)(2,1)}, u32[]{:S(2)}) copy-start(bf16[8192,64]{1,0:T(8,128)(2,1)} %get-tuple-element.45) | copy-start | bytes 3145732
  89.4 48.5 %copy-start.4 = (f32[1024]{0:T(1024)S(1)}, f32[1024]{0:T(1024)}, u32[]{:S(2)}) copy-start(f32[1024]{0:T(1024)} %get-tuple-element.57) | copy-start | bytes 12292
  138.7 9.9 %copy-start.1 = (f32[1024,1]{1,0:T(8,128)}, f32[1024,1]{1,0:T(8,128)S(1)}, u32[]{:S(2)}) copy-start(f32[1024,1]{1,0:T(8,128)S(1)} %copy.99.ra_ref) | copy-start | bytes 12292
  178.9 91.5 %reduce-scatter.2.cloned.1.call-start = ((), (), s32[]{:S(2)}) async-start(), calls=%async_computation.1 | async-start | bytes 1179648 | tf_op jit(solution)/shard_map/reduce_scatter | solution.py:231
  184.2 35.6 %copy-start.3 = (f32[8192]{0:T(1024)S(1)}, f32[8192]{0:T(1024)}, u32[]{:S(2)}) copy-start(f32[8192]{0:T(1024)} %copy-done.2) | copy-start | bytes 98308
  220.5 50.8 %copy-start.6 = (f32[64]{0:T(128)S(1)}, f32[64]{0:T(128)}, u32[]{:S(2)}) copy-start(f32[64]{0:T(128)} %param.17) | copy-start | bytes 772
Sparse Core Ops, SparseCore 0:
  38.9 26.7 all-gather.7
  179.0 36.9 all-gather.9
  237.2 33.1 reduce-scatter.1

commit v5 on v2

--- a/solution.py
+++ b/solution.py
@@ -50,9 +50,11 @@
     out_ref[...] = m + jnp.log(l)
 
 
-def row_lse(qa, yat, rb, cb, ra, ca, tm=128, tn=512):
+def row_lse(qa, yat, rb, cb, ra, ca, tm=512, tn=2048):
     nr, kq = qa.shape
     n = yat.shape[1]
+    tm = min(tm, nr)
+    tn = min(tn, n)
     return pl.pallas_call(
         functools.partial(_row_lse_kernel, tn=tn),
         grid=(nr // tm,),
@@ -92,9 +94,11 @@
     out_ref[...] = m + jnp.log(l)
 
 
-def col_lse(qa, yat, rb, cb, ra, ca, tm=128, tn=512):
+def col_lse(qa, yat, rb, cb, ra, ca, tm=512, tn=1024):
     nr, kq = qa.shape
     n = yat.shape[1]
+    tm = min(tm, nr)
+    tn = min(tn, n)
     return pl.pallas_call(
         functools.partial(_col_lse_kernel, tm=tm),
         grid=(n // tn,),
@@ -130,9 +134,11 @@
     out_ref[...] = acc
 
 
-def moments(qa, yat, rb, cb, ra, ca, feats, tm=128, tn=512):
+def moments(qa, yat, rb, cb, ra, ca, feats, tm=512, tn=2048):
     nr, kq = qa.shape
     n = yat.shape[1]
+    tm = min(tm, nr)
+    tn = min(tn, n)
     nf = feats.shape[1]
     return pl.pallas_call(
         functools.partial(_moment_kernel, tn=tn),

time: 343 us -> 264 us (0.77)
  Pallas kernels: 130 us -> 51.2 us
    pallas_call x1, Pallas kernels: 48.9 us -> 17.1 us  [row_lse(): pl.pallas_call(functools.partial(_row_lse_kernel, tn=tn), grid=(nr // tm,...]
    pallas_call x1, Pallas kernels: 46.4 us -> 16.5 us  [moments(): pl.pallas_call(functools.partial(_moment_kernel, tn=tn), grid=(nr // tm,)...]
    pallas_call x1, Pallas kernels: 34.8 us -> 17.6 us  [col_lse(): pl.pallas_call(functools.partial(_col_lse_kernel, tm=tm), grid=(n // tn,)...]
  transfers between devices with their start and end apart: 3 -> 3, of which waited for: 3 -> 3; matrix products, arithmetic and copies ran while one was open for 4% -> 5% of each run, Pallas kernels for 0% -> 0%
where the time goes in v5:
time: 264 us; the launch traced here: 263 us
  waiting for transfers between devices  85 us (32%)
  blocking collectives  63 us (24%)
  Pallas kernels  51.2 us (19%)
  other arithmetic  26 us (10%)
  local copies, waits for them, and re-layouts  21.9 us (8%)
  between operations  15.9 us (6%)
    all_gather x2, waiting for transfers between devices, gather_row(): return lax.all_gather(inner, ROW[0], axis=0, tiled=True)  51.7 us
    reduce_scatter x1, waiting for transfers between devices, on_device(): own = lax.psum_scatter(both, COL, scatter_dimension=0, tiled=True)  33.3 us
    all_gather x2, blocking collectives, gather_row(): inner = lax.all_gather(value, ROW[1], axis=0, tiled=True)  25.3 us
    unnamed x1, blocking collectives  24.1 us
    pallas_call x1, Pallas kernels, col_lse(): pl.pallas_call(functools.partial(_col_lse_kernel, tm=tm), grid=(n // tn,)...  17.6 us
    pallas_call x1, Pallas kernels, row_lse(): pl.pallas_call(functools.partial(_row_lse_kernel, tn=tn), grid=(nr // tm,...  17.1 us
    pallas_call x1, Pallas kernels, moments(): pl.pallas_call(functools.partial(_moment_kernel, tn=tn), grid=(nr // tm,)...  16.5 us
    all_gather x1, blocking collectives, gather_col(): return lax.all_gather(value, COL, axis=0, tiled=True)  13.6 us
  transfers between devices with their start and end apart: 3, of which 3 were waited for; matrix products, arithmetic and copies ran while one was open for 5% of the time, Pallas kernels for 0%

profile of v5, /device:TPU:2, one launch (start us, length us, event | category | flops | bytes accessed | tf_op | source)
XLA Modules:
  0.0 263.1 jit_solution(1591910316214526212)
XLA Ops:
  7.2 0.8 copy.107
  9.5 0.9 copy.109
  10.5 13.3 %all_gather.19 = bf16[1024,67]{1,0:T(8,128)(2,1)} all-gather(bf16[256,67]{1,0:T(8,128)(2,1)S(1)} %fusion.18), channel_id=1, replica_groups=mesh['z'=8,'x'=4,'y'=4,'core'=2] {'x'}, dimensions={0}, use_global_device_ids=true | all-gather | bytes 171520 | tf_op jit(solution)/shard_map/all_gather | solution.py:19
  23.9 0.8 copy.106
  24.7 0.8 copy.105
  25.7 13.6 %all_gather.18 = bf16[1024,129]{1,0:T(8,128)(2,1)S(1)} all-gather(bf16[128,129]{1,0:T(8,128)(2,1)S(1)} %pad_maximum_fusion.2), channel_id=1, replica_groups=mesh['z'=8,'x'=4,'y'=4,'core'=2] {'y','core'}, dimensions={0}, use_global_device_ids=true | all-gather | bytes 297216 | tf_op jit(solution)/shard_map/all_gather | solution.py:24
  39.3 1.2 fusion.5
  40.5 1.0 copy.113.rb_ref
  41.6 1.1 copy.114.ra_ref
  42.7 1.3 dynamic-slice.7
  44.8 0.9 pad_maximum_fusion.1.qa_ref
  45.7 21.9 %all-gather.6.cloned.1.call-done = bf16[8192,67]{1,0:T(8,128)(2,1)} async-done(((bf16[1024,67]{1,0:T(8,128)(2,1)}), bf16[8192,67]{1,0:T(8,128)(2,1)}) %all-gather.6.cloned.1.call-update) | async-done | bytes 1097744 | tf_op jit(solution)/shard_map/all_gather | solution.py:20
  67.6 3.5 %fusion.19 = (bf16[8192,64]{1,0:T(8,128)(2,1)}, bf16[64,8192]{0,1:T(8,128)(2,1)S(1)}) fusion(bf16[8192,67]{1,0:T(8,128)(2,1)} %all-gather.6.cloned.1.call-done), kind=kLoop, calls=%fused_computation.58 | loop fusion | bytes 3145728 | tf_op jit(solution)/shard_map/slice | solution.py:180
  71.1 2.5 pad_maximum_fusion
  73.6 4.1 %copy.112.yat_ref = bf16[128,8192]{1,0:T(8,128)(2,1)} copy(bf16[128,8192]{0,1:T(8,128)(2,1)} %pad_maximum_fusion) | data formatting | bytes 4194304 | tf_op jit(solution)/shard_map/concatenate | solution.py:194
  77.7 2.4 fusion.1
  80.7 5.1 %convert_reduce_fusion.1 = (f32[]{:T(128)}, f32[]{:T(128)}, f32[8192]{0:T(1024)S(1)}, f32[8192]{0:T(1024)S(1)}) fusion(bf16[8192,67]{1,0:T(8,128)(2,1)S(1)} %copy-done), kind=kLoop, calls=%fused_computation.9 | loop fusion | flops 49150 | bytes 114696 | tf_op jit(solution)/shard_map/reduce_sum | solution.py:183
  86.4 17.1 %shard_map.103 = f32[1024,1]{1,0:T(8,128)} custom-call(bf16[1024,128]{1,0:T(8,128)(2,1)} %pad_maximum_fusion.1.qa_ref, bf16[128,8192]{1,0:T(8,128)(2,1)} %copy.112.yat_ref, f32[1024,1]{1,0:T(8,128)} %copy.113.rb_ref, f32[1,8192]{1,0:T(1,128)} %bitcast.19, f32[1024,1]{1,0:T(8,128)} %copy.114.ra_ref, f32[1,8192]{1,0:T(1,128)} %add_add_fusion.ca_ref), custom_call_target="tpu_custom_call" | custom-call | tf_op jit(solution)/shard_map/pallas_call | solution.py:58
  103.5 1.4 reduce.9
  104.9 1.4 concatenate.25
  106.6 24.1 %all-reduce.1 = f32[8208]{0:T(1024)S(1)} all-reduce(f32[8208]{0:T(1024)S(1)} %dynamic-update-slice.3), channel_id=2, replica_groups=mesh['z'=8,'x'=4,'y'=4,'core'=2] {'y','core'}, use_global_device_ids=true, to_apply=%add.1 | all-reduce | flops 8208 | bytes 65664
  133.7 1.0 log_add_fusion.ra_ref
  134.7 17.6 %shard_map.104 = f32[1,8192]{1,0:T(1,128)} custom-call(bf16[1024,128]{1,0:T(8,128)(2,1)} %pad_maximum_fusion.1.qa_ref, bf16[128,8192]{1,0:T(8,128)(2,1)} %copy.112.yat_ref, f32[1024,1]{1,0:T(8,128)} %copy.113.rb_ref, f32[1,8192]{1,0:T(1,128)} %bitcast.20, f32[1024,1]{1,0:T(8,128)} %log_add_fusion.ra_ref, f32[1,8192]{1,0:T(1,128)} %bitcast.23), custom_call_target="tpu_custom_call" | custom-call | tf_op jit(solution)/shard_map/pallas_call | solution.py:102
  152.3 12.0 %all-gather.1 = f32[4,1,8192]{2,1,0:T(1,128)S(1)} all-gather(f32[1,1,8192]{2,1,0:T(1,128)} %bitcast.28), channel_id=1, replica_groups=mesh['z'=8,'x'=4,'y'=4,'core'=2] {'x'}, dimensions={0}, use_global_device_ids=true | all-gather | bytes 163840 | tf_op jit(solution)/shard_map/all_gather | solution.py:19
  165.1 4.7 %maximum_maximum_fusion.f_ref = bf16[8192,256]{1,0:T(8,128)(2,1)} fusion(bf16[8192,64]{1,0:T(8,128)(2,1)} %get-tuple-element.46, bf16[8192,64]{1,0:T(8,128)(2,1)S(1)} %copy-done.1, bf16[256]{0:T(256)(128)(2,1)S(1)} %pad.6.clone, bf16[256]{0:T(256)(128)(2,1)S(1)} %pad.5.clone), kind=kLoop, calls=%fused_computation.8 | loop fusion | flops 16777216 | bytes 6292480 | tf_op jit(solution)/shard_map/concatenate | solution.py:196
  169.8 29.7 %all-gather.8.cloned.1.call-done = f32[8,4,8192]{2,1,0:T(4,128)} async-done(((f32[1,4,8192]{2,1,0:T(4,128)}), f32[8,4,8192]{2,1,0:T(4,128)}) %all-gather.8.cloned.1.call-update) | async-done | bytes 1048592 | tf_op jit(solution)/shard_map/all_gather | solution.py:20
  199.5 1.6 reshape.222
  201.1 1.4 reduce_max.19
  204.1 16.5 %shard_map.105 = f32[1024,256]{1,0:T(8,128)} custom-call(bf16[1024,128]{1,0:T(8,128)(2,1)} %pad_maximum_fusion.1.qa_ref, bf16[128,8192]{1,0:T(8,128)(2,1)} %copy.112.yat_ref, f32[1024,1]{1,0:T(8,128)} %copy.113.rb_ref, f32[1,8192]{1,0:T(1,128)} %bitcast.21, f32[1024,1]{1,0:T(8,128)} %copy-done.2, f32[1,8192]{1,0:T(1,128)} %add_subtract_fusion.ca_ref, ...), custom_call_target="tpu_custom_call" | custom-call | tf_op jit(solution)/shard_map/pallas_call | solution.py:143
  220.6 33.3 %reduce-scatter.2.cloned.1.call-done = f32[128,129]{1,0:T(8,128)} async-done(((f32[1024,129]{1,0:T(8,128)}), f32[128,129]{1,0:T(8,128)}) %reduce-scatter.2.cloned.1.call-update) | async-done | bytes 66064 | tf_op jit(solution)/shard_map/reduce_scatter | solution.py:225
  253.9 0.9 slice_reduce_fusion
  254.9 1.0 fusion.11
  (45 shorter events, 8.3 us)
Async XLA Ops:
  7.2 60.4 %all-gather.6.cloned.1.call-start = ((), (), s32[]{:S(2)}) async-start(), calls=%async_computation.1 | async-start | bytes 2359296 | tf_op jit(solution)/shard_map/all_gather | solution.py:20
  23.8 175.7 %all-gather.8.cloned.1.call-start = ((), (), s32[]{:S(2)}) async-start(), calls=%async_computation.3 | async-start | bytes 1179648 | tf_op jit(solution)/shard_map/all_gather | solution.py:20
  71.1 6.6 %copy-start = (bf16[8192,67]{1,0:T(8,128)(2,1)S(1)}, bf16[8192,67]{1,0:T(8,128)(2,1)}, u32[]{:S(2)}) copy-start(bf16[8192,67]{1,0:T(8,128)(2,1)} %all-gather.6.cloned.1.call-done) | copy-start | bytes 3293188
  71.1 6.6 %copy-start.5 = (f32[64]{0:T(128)S(1)}, f32[64]{0:T(128)}, u32[]{:S(2)}) copy-start(f32[64]{0:T(128)} %param.16) | copy-start | bytes 772
  80.7 22.8 %copy-start.3 = (f32[8192]{0:T(1024)}, f32[8192]{0:T(1024)S(1)}, u32[]{:S(2)}) copy-start(f32[8192]{0:T(1024)S(1)} %get-tuple-element.55) | copy-start | bytes 98308
  103.5 61.6 %copy-start.1 = (bf16[8192,64]{1,0:T(8,128)(2,1)S(1)}, bf16[8192,64]{1,0:T(8,128)(2,1)}, u32[]{:S(2)}) copy-start(bf16[8192,64]{1,0:T(8,128)(2,1)} %get-tuple-element.44) | copy-start | bytes 3145732
  133.7 36.1 %copy-start.2 = (f32[1024,1]{1,0:T(8,128)}, f32[1024,1]{1,0:T(8,128)S(1)}, u32[]{:S(2)}) copy-start(f32[1024,1]{1,0:T(8,128)S(1)} %copy.116.ra_ref) | copy-start | bytes 12292
  165.1 88.8 %reduce-scatter.2.cloned.1.call-start = ((), (), s32[]{:S(2)}) async-start(), calls=%async_computation.2 | async-start | bytes 1179648 | tf_op jit(solution)/shard_map/reduce_scatter | solution.py:225
  169.8 33.6 %copy-start.4 = (f32[8192]{0:T(1024)S(1)}, f32[8192]{0:T(1024)}, u32[]{:S(2)}) copy-start(f32[8192]{0:T(1024)} %copy-done.3) | copy-start | bytes 98308
  204.0 50.8 %copy-start.6 = (f32[64]{0:T(128)S(1)}, f32[64]{0:T(128)}, u32[]{:S(2)}) copy-start(f32[64]{0:T(128)} %param.17) | copy-start | bytes 772
Sparse Core Ops, SparseCore 0:
  24.0 43.5 all-gather.5
  165.2 34.3 all-gather.7
  220.7 33.1 reduce-scatter.1

commit v6 on v5

--- a/solution.py
+++ b/solution.py
@@ -6,6 +6,7 @@
 from jax.experimental import pallas as pl
 from jax.sharding import Mesh, PartitionSpec as P
 
+
 EPS = 0.5
 KAPPA = 0.5
 RIDGE = 1.0
@@ -21,7 +22,8 @@
 
 
 def gather_col(value):
-    return lax.all_gather(value, COL, axis=0, tiled=True)
+    inner = lax.all_gather(value, COL[1], axis=0, tiled=True)
+    return lax.all_gather(inner, COL[0], axis=0, tiled=True)
 
 
 KF = 256
@@ -163,11 +165,11 @@
     return top + jnp.log(jnp.sum(jnp.exp(parts - top[None, :]), axis=0))
 
 
-def on_device(x_points, y_points, row_mass, col_mass, multipliers, col_potential, basket, damping):
+def sweep(x_points, y_points, row_mass, col_mass, multipliers, col_potential, basket, damping):
     width = x_points.shape[1]
     share = x_points.shape[0]
     x_pack = jnp.concatenate([x_points, multipliers, row_mass[:, None]], axis=1)
-    x_rows_pack = gather_col(x_pack)
+    x_rows_pack = lax.all_gather(x_pack, COL, axis=0, tiled=True)
     x_rows = x_rows_pack[:, :width]
     mult_rows = x_rows_pack[:, width : 2 * width]
     mass_rows = x_rows_pack[:, 2 * width]
@@ -247,7 +249,7 @@
         P(),
     )
     return jax.shard_map(
-        on_device,
+        sweep,
         mesh=split,
         in_specs=placed,
         out_specs=(P(ROW), P(COL), P(ROW + COL, None)),

time: 264 us -> 257 us (0.973)
  blocking collectives: 63 us -> 54.7 us
    unnamed x1, blocking collectives: 24.1 us -> 3.28 us
    all_gather x1 -> x2, blocking collectives: 13.6 us -> 25.9 us  [the longest x1 13.6 us: sweep(): x_rows_pack = lax.all_gather(x_pack, COL, axis=0, tiled=True)]
    unnamed x23 -> x25, local copies, waits for them, and re-layouts: 7.12 us -> 7.21 us
where the time goes in v6:
time: 257 us
  waiting for transfers between devices  86.8 us (34%)
  blocking collectives  54.7 us (21%)
  Pallas kernels  51.2 us (20%)
  other arithmetic  26 us (10%)
  local copies, waits for them, and re-layouts  21.9 us (9%)
  between operations  15.9 us (6%)
    all_gather x2, waiting for transfers between devices, gather_row(): return lax.all_gather(inner, ROW[0], axis=0, tiled=True)  53.4 us
    reduce_scatter x1, waiting for transfers between devices, sweep(): own = lax.psum_scatter(both, COL, scatter_dimension=0, tiled=True)  33.3 us
    all_gather x2, blocking collectives, gather_row(): inner = lax.all_gather(value, ROW[1], axis=0, tiled=True)  25.5 us
    pallas_call x1, Pallas kernels, col_lse(): pl.pallas_call(functools.partial(_col_lse_kernel, tm=tm), grid=(n // tn,)...  17.6 us
    pallas_call x1, Pallas kernels, row_lse(): pl.pallas_call(functools.partial(_row_lse_kernel, tn=tn), grid=(nr // tm,...  17.1 us
    pallas_call x1, Pallas kernels, moments(): pl.pallas_call(functools.partial(_moment_kernel, tn=tn), grid=(nr // tm,)...  16.5 us
    all_gather x1, blocking collectives, sweep(): x_rows_pack = lax.all_gather(x_pack, COL, axis=0, tiled=True)  13.6 us
    all_gather x1, blocking collectives, gather_col(): return lax.all_gather(inner, COL[0], axis=0, tiled=True)  12.3 us
  transfers between devices with their start and end apart: 3, of which 3 were waited for; matrix products, arithmetic and copies ran while one was open for 5% of the time, Pallas kernels for 0%

profile of v6, /device:TPU:2, one launch (start us, length us, event | category | flops | bytes accessed | tf_op | source)
XLA Modules:
  0.0 256.6 jit_solution(11412086708072601579)
XLA Ops:
  9.5 0.9 copy.65
  10.5 13.3 %all_gather.22 = bf16[1024,67]{1,0:T(8,128)(2,1)} all-gather(bf16[256,67]{1,0:T(8,128)(2,1)S(1)} %fusion.18), channel_id=1, replica_groups=mesh['z'=8,'x'=4,'y'=4,'core'=2] {'x'}, dimensions={0}, use_global_device_ids=true | all-gather | bytes 171520 | tf_op jit(solution)/shard_map/all_gather | solution.py:20
  23.9 0.8 copy.62
  24.7 0.8 copy.61
  25.7 13.6 %all_gather.21 = bf16[1024,129]{1,0:T(8,128)(2,1)S(1)} all-gather(bf16[128,129]{1,0:T(8,128)(2,1)S(1)} %pad_maximum_fusion.2), channel_id=1, replica_groups=mesh['z'=8,'x'=4,'y'=4,'core'=2] {'y','core'}, dimensions={0}, use_global_device_ids=true | all-gather | bytes 297216 | tf_op jit(solution)/shard_map/all_gather | solution.py:172
  39.3 1.2 fusion.5
  40.5 1.0 copy.69.rb_ref
  41.6 1.1 copy.70.ra_ref
  42.7 1.3 dynamic-slice.7
  44.8 0.9 pad_maximum_fusion.1.qa_ref
  45.7 21.9 %all-gather.7.cloned.1.call-done = bf16[8192,67]{1,0:T(8,128)(2,1)} async-done(((bf16[1024,67]{1,0:T(8,128)(2,1)}), bf16[8192,67]{1,0:T(8,128)(2,1)}) %all-gather.7.cloned.1.call-update) | async-done | bytes 1097744 | tf_op jit(solution)/shard_map/all_gather | solution.py:21
  67.6 3.5 %fusion.19 = (bf16[8192,64]{1,0:T(8,128)(2,1)}, bf16[64,8192]{0,1:T(8,128)(2,1)S(1)}) fusion(bf16[8192,67]{1,0:T(8,128)(2,1)} %all-gather.7.cloned.1.call-done), kind=kLoop, calls=%fused_computation.58 | loop fusion | bytes 3145728 | tf_op jit(solution)/shard_map/slice | solution.py:182
  71.1 2.5 pad_maximum_fusion
  73.6 4.1 %copy.68.yat_ref = bf16[128,8192]{1,0:T(8,128)(2,1)} copy(bf16[128,8192]{0,1:T(8,128)(2,1)} %pad_maximum_fusion) | data formatting | bytes 4194304 | tf_op jit(solution)/shard_map/concatenate | solution.py:196
  77.7 2.4 fusion.1
  80.7 5.1 %convert_reduce_fusion.1 = (f32[]{:T(128)}, f32[]{:T(128)}, f32[8192]{0:T(1024)S(1)}, f32[8192]{0:T(1024)S(1)}) fusion(bf16[8192,67]{1,0:T(8,128)(2,1)S(1)} %copy-done), kind=kLoop, calls=%fused_computation.9 | loop fusion | flops 49150 | bytes 114696 | tf_op jit(solution)/shard_map/reduce_sum | solution.py:185
  86.4 17.1 %shard_map.103 = f32[1024,1]{1,0:T(8,128)} custom-call(bf16[1024,128]{1,0:T(8,128)(2,1)} %pad_maximum_fusion.1.qa_ref, bf16[128,8192]{1,0:T(8,128)(2,1)} %copy.68.yat_ref, f32[1024,1]{1,0:T(8,128)} %copy.69.rb_ref, f32[1,8192]{1,0:T(1,128)} %bitcast.19, f32[1024,1]{1,0:T(8,128)} %copy.70.ra_ref, f32[1,8192]{1,0:T(1,128)} %add_add_fusion.ca_ref), custom_call_target="tpu_custom_call" | custom-call | tf_op jit(solution)/shard_map/pallas_call | solution.py:60
  103.5 1.4 reduce.9
  104.9 1.4 concatenate.25
  106.6 3.3 %all-reduce.1 = f32[2052]{0:T(1024)S(1)} all-reduce(f32[2052]{0:T(1024)S(1)} %dynamic-update-slice.3), channel_id=2, replica_groups=mesh['z'=8,'x'=4,'y'=4,'core'=2] {'core'}, use_global_device_ids=true, to_apply=%add.1 | all-reduce | flops 2052 | bytes 16416
  109.9 12.3 %all-gather.1 = f32[4,2,1026]{2,1,0:T(2,128)S(1)} all-gather(f32[1,2,1026]{2,1,0:T(2,128)S(1)} %reshape.219), channel_id=1, replica_groups=mesh['z'=8,'x'=4,'y'=4,'core'=2] {'y'}, dimensions={0}, use_global_device_ids=true | all-gather | bytes 41040 | tf_op jit(solution)/shard_map/all_gather | solution.py:26
  125.2 1.0 log_add_fusion.ra_ref
  126.2 17.6 %shard_map.104 = f32[1,8192]{1,0:T(1,128)} custom-call(bf16[1024,128]{1,0:T(8,128)(2,1)} %pad_maximum_fusion.1.qa_ref, bf16[128,8192]{1,0:T(8,128)(2,1)} %copy.68.yat_ref, f32[1024,1]{1,0:T(8,128)} %copy.69.rb_ref, f32[1,8192]{1,0:T(1,128)} %bitcast.20, f32[1024,1]{1,0:T(8,128)} %log_add_fusion.ra_ref, f32[1,8192]{1,0:T(1,128)} %bitcast.23), custom_call_target="tpu_custom_call" | custom-call | tf_op jit(solution)/shard_map/pallas_call | solution.py:104
  143.8 12.2 %all-gather.2 = f32[4,1,8192]{2,1,0:T(1,128)S(1)} all-gather(f32[1,1,8192]{2,1,0:T(1,128)} %bitcast.28), channel_id=1, replica_groups=mesh['z'=8,'x'=4,'y'=4,'core'=2] {'x'}, dimensions={0}, use_global_device_ids=true | all-gather | bytes 163840 | tf_op jit(solution)/shard_map/all_gather | solution.py:20
  156.8 4.7 %maximum_maximum_fusion.f_ref = bf16[8192,256]{1,0:T(8,128)(2,1)} fusion(bf16[8192,64]{1,0:T(8,128)(2,1)} %get-tuple-element.40, bf16[8192,64]{1,0:T(8,128)(2,1)S(1)} %copy-done.1, bf16[256]{0:T(256)(128)(2,1)S(1)} %pad.6.clone, bf16[256]{0:T(256)(128)(2,1)S(1)} %pad.5.clone), kind=kLoop, calls=%fused_computation.8 | loop fusion | flops 16777216 | bytes 6292480 | tf_op jit(solution)/shard_map/concatenate | solution.py:198
  161.5 31.5 %all-gather.9.cloned.1.call-done = f32[8,4,8192]{2,1,0:T(4,128)} async-done(((f32[1,4,8192]{2,1,0:T(4,128)}), f32[8,4,8192]{2,1,0:T(4,128)}) %all-gather.9.cloned.1.call-update) | async-done | bytes 1048592 | tf_op jit(solution)/shard_map/all_gather | solution.py:21
  193.0 1.6 reshape.224
  194.6 1.4 reduce_max.19
  197.5 16.5 %shard_map.105 = f32[1024,256]{1,0:T(8,128)} custom-call(bf16[1024,128]{1,0:T(8,128)(2,1)} %pad_maximum_fusion.1.qa_ref, bf16[128,8192]{1,0:T(8,128)(2,1)} %copy.68.yat_ref, f32[1024,1]{1,0:T(8,128)} %copy.69.rb_ref, f32[1,8192]{1,0:T(1,128)} %bitcast.21, f32[1024,1]{1,0:T(8,128)} %copy-done.2, f32[1,8192]{1,0:T(1,128)} %add_subtract_fusion.ca_ref, ...), custom_call_target="tpu_custom_call" | custom-call | tf_op jit(solution)/shard_map/pallas_call | solution.py:145
  214.1 33.3 %reduce-scatter.2.cloned.1.call-done = f32[128,129]{1,0:T(8,128)} async-done(((f32[1024,129]{1,0:T(8,128)}), f32[128,129]{1,0:T(8,128)}) %reduce-scatter.2.cloned.1.call-update) | async-done | bytes 66064 | tf_op jit(solution)/shard_map/reduce_scatter | solution.py:227
  247.4 0.9 slice_reduce_fusion
  248.3 1.0 fusion.11
  (47 shorter events, 9.1 us)
Async XLA Ops:
  7.2 60.4 %all-gather.7.cloned.1.call-start = ((), (), s32[]{:S(2)}) async-start(), calls=%async_computation.1 | async-start | bytes 2359296 | tf_op jit(solution)/shard_map/all_gather | solution.py:21
  23.8 169.2 %all-gather.9.cloned.1.call-start = ((), (), s32[]{:S(2)}) async-start(), calls=%async_computation.3 | async-start | bytes 1179648 | tf_op jit(solution)/shard_map/all_gather | solution.py:21
  71.1 6.6 %copy-start = (bf16[8192,67]{1,0:T(8,128)(2,1)S(1)}, bf16[8192,67]{1,0:T(8,128)(2,1)}, u32[]{:S(2)}) copy-start(bf16[8192,67]{1,0:T(8,128)(2,1)} %all-gather.7.cloned.1.call-done) | copy-start | bytes 3293188
  71.1 6.6 %copy-start.5 = (f32[64]{0:T(128)S(1)}, f32[64]{0:T(128)}, u32[]{:S(2)}) copy-start(f32[64]{0:T(128)} %param.16) | copy-start | bytes 772
  80.7 22.8 %copy-start.3 = (f32[8192]{0:T(1024)}, f32[8192]{0:T(1024)S(1)}, u32[]{:S(2)}) copy-start(f32[8192]{0:T(1024)S(1)} %get-tuple-element.49) | copy-start | bytes 98308
  103.5 53.3 %copy-start.1 = (bf16[8192,64]{1,0:T(8,128)(2,1)S(1)}, bf16[8192,64]{1,0:T(8,128)(2,1)}, u32[]{:S(2)}) copy-start(bf16[8192,64]{1,0:T(8,128)(2,1)} %get-tuple-element.38) | copy-start | bytes 3145732
  125.2 36.3 %copy-start.2 = (f32[1024,1]{1,0:T(8,128)}, f32[1024,1]{1,0:T(8,128)S(1)}, u32[]{:S(2)}) copy-start(f32[1024,1]{1,0:T(8,128)S(1)} %copy.71.ra_ref) | copy-start | bytes 12292
  156.8 90.6 %reduce-scatter.2.cloned.1.call-start = ((), (), s32[]{:S(2)}) async-start(), calls=%async_computation.2 | async-start | bytes 1179648 | tf_op jit(solution)/shard_map/reduce_scatter | solution.py:227
  161.5 35.3 %copy-start.4 = (f32[8192]{0:T(1024)S(1)}, f32[8192]{0:T(1024)}, u32[]{:S(2)}) copy-start(f32[8192]{0:T(1024)} %copy-done.3) | copy-start | bytes 98308
  197.5 50.8 %copy-start.6 = (f32[64]{0:T(128)S(1)}, f32[64]{0:T(128)}, u32[]{:S(2)}) copy-start(f32[64]{0:T(128)} %param.17) | copy-start | bytes 772
Sparse Core Ops, SparseCore 0:
  24.0 43.5 all-gather.6
  156.9 36.0 all-gather.8
  214.2 33.1 reduce-scatter.1

commit v7 on v6

--- a/solution.py
+++ b/solution.py
@@ -19,11 +19,6 @@
 def gather_row(value):
     inner = lax.all_gather(value, ROW[1], axis=0, tiled=True)
     return lax.all_gather(inner, ROW[0], axis=0, tiled=True)
-
-
-def gather_col(value):
-    inner = lax.all_gather(value, COL[1], axis=0, tiled=True)
-    return lax.all_gather(inner, COL[0], axis=0, tiled=True)
 
 
 KF = 256
@@ -186,12 +181,13 @@
 
     xf = x_rows.astype(jnp.float32)
     hf = mult_rows.astype(jnp.float32)
-    yf = y_cols.astype(jnp.float32)
     row_term2 = 2.0 * (-jnp.sum(hf * xf, axis=1) - KAPPA / width * jnp.sum(xf * xf, axis=1))
     row_basket2 = 2.0 * jnp.sum(xf * basket[None, :], axis=1)
+    q_core = jnp.concatenate([mult_rows * 2, x_rows * (2.0 * KAPPA / width * 2.0)], axis=1)
+    log_row = jnp.log(mass_rows.astype(jnp.float32))
+    yf = y_cols.astype(jnp.float32)
     col_term2 = 2.0 * (-(KAPPA / width) * jnp.sum(yf * yf, axis=1))
     col_basket2 = 2.0 * jnp.sum(yf * basket[None, :], axis=1)
-    q_core = jnp.concatenate([mult_rows * 2, x_rows * (2.0 * KAPPA / width * 2.0)], axis=1)
     y_t = y_cols.T
     y_core_t = jnp.concatenate([y_t, y_t], axis=0)
     ny_cols = y_cols.shape[0]
@@ -200,8 +196,6 @@
          jnp.zeros((ny_cols, KF - 2 * width - 1), jnp.float32)], axis=1
     ).astype(jnp.bfloat16)
 
-    row_weight = mass_rows.astype(jnp.float32)
-    log_row = jnp.log(row_weight)
     log_col = jnp.log(mass_cols)
     nrows = x_rows.shape[0]
 
@@ -209,7 +203,9 @@
     row_local = row_lse(q_core, y_core_t, row_basket2, col_basket2, row_term2, gshift)
     nu_part = jnp.sum(mass_cols)
     row_msg = jnp.concatenate([row_local, jnp.stack([nu_part, rmass_part])])
-    row_all = gather_col(row_msg[None, :])
+    row_core = lax.all_gather(row_msg, COL[1], axis=0)
+    row_msg = jnp.concatenate([merge_lse(row_core[:, :nrows]), jnp.sum(row_core[:, nrows:], axis=0)])
+    row_all = lax.all_gather(row_msg, COL[0], axis=0)
     nu_total = jnp.sum(row_all[:, nrows])
     mu_total = jnp.sum(row_all[:, nrows + 1])
     log_nu_total = jnp.log(nu_total)
@@ -217,7 +213,8 @@
     fshift = row_term2 + row_potential / EPS + log_row
 
     col_local = col_lse(q_core, y_core_t, row_basket2, col_basket2, fshift, col_term2)
-    col_all = gather_row(col_local[None, :])
+    col_x = merge_lse(lax.all_gather(col_local, ROW[1], axis=0))
+    col_all = lax.all_gather(col_x, ROW[0], axis=0)
     col_potential_new = -EPS * (merge_lse(col_all) - jnp.log(mu_total))
     gq = col_term2 + col_potential_new / EPS + log_col - log_nu_total
     fq = row_term2 + row_potential / EPS

time: 257 us -> 251 us (0.977)
  waiting for transfers between devices: 86.8 us -> 51.6 us
  blocking collectives: 54.7 us -> 84.2 us
    all_gather x2 -> x1, waiting for transfers between devices: 53.4 us -> 19.8 us  [gather_row(): return lax.all_gather(inner, ROW[0], axis=0, tiled=True)]
    all_gather x1 -> x2, blocking collectives: 12.3 us -> 37 us  [the longest x1 24.8 us: sweep(): col_all = lax.all_gather(col_x, ROW[0], axis=0)]
    unnamed x1 -> x2, blocking collectives: 3.28 us -> 20.3 us
    all_gather x2 -> x1, blocking collectives: 25.5 us -> 13.3 us  [gather_row(): inner = lax.all_gather(value, ROW[1], axis=0, tiled=True)]
    unnamed x25 -> x23, local copies, waits for them, and re-layouts: 7.21 us -> 6.04 us
  transfers between devices with their start and end apart: 3 -> 2, of which waited for: 3 -> 2; matrix products, arithmetic and copies ran while one was open for 5% -> 4% of each run, Pallas kernels for 0% -> 0%
where the time goes in v7:
time: 251 us; the launch traced here: 250 us
  blocking collectives  84.2 us (34%)
  waiting for transfers between devices  51.6 us (21%)
  Pallas kernels  51.2 us (20%)
  other arithmetic  25.1 us (10%)
  local copies, waits for them, and re-layouts  20.9 us (8%)
  between operations  16.9 us (7%)
    reduce_scatter x1, waiting for transfers between devices, sweep(): own = lax.psum_scatter(both, COL, scatter_dimension=0, tiled=True)  31.7 us
    all_gather x1, blocking collectives, sweep(): col_all = lax.all_gather(col_x, ROW[0], axis=0)  24.8 us
    unnamed x2, blocking collectives  20.3 us
    all_gather x1, waiting for transfers between devices, gather_row(): return lax.all_gather(inner, ROW[0], axis=0, tiled=True)  19.8 us
    pallas_call x1, Pallas kernels, col_lse(): pl.pallas_call(functools.partial(_col_lse_kernel, tm=tm), grid=(n // tn,)...  17.6 us
    pallas_call x1, Pallas kernels, row_lse(): pl.pallas_call(functools.partial(_row_lse_kernel, tn=tn), grid=(nr // tm,...  17.1 us
    pallas_call x1, Pallas kernels, moments(): pl.pallas_call(functools.partial(_moment_kernel, tn=tn), grid=(nr // tm,)...  16.5 us
    all_gather x1, blocking collectives, sweep(): x_rows_pack = lax.all_gather(x_pack, COL, axis=0, tiled=True)  13.6 us
  transfers between devices with their start and end apart: 2, of which 2 were waited for; matrix products, arithmetic and copies ran while one was open for 4% of the time, Pallas kernels for 0%

profile of v7, /device:TPU:2, one launch (start us, length us, event | category | flops | bytes accessed | tf_op | source)
XLA Modules:
  0.0 249.9 jit_solution(3218321785244524766)
XLA Ops:
  7.2 0.8 copy.104
  9.5 0.9 copy.106
  10.5 13.3 %all_gather.29 = bf16[1024,67]{1,0:T(8,128)(2,1)} all-gather(bf16[256,67]{1,0:T(8,128)(2,1)S(1)} %fusion.20), channel_id=1, replica_groups=mesh['z'=8,'x'=4,'y'=4,'core'=2] {'x'}, dimensions={0}, use_global_device_ids=true | all-gather | bytes 171520 | tf_op jit(solution)/shard_map/all_gather | solution.py:20
  23.9 0.8 copy.103
  24.7 0.8 copy.102
  25.7 13.6 %all_gather.28 = bf16[1024,129]{1,0:T(8,128)(2,1)S(1)} all-gather(bf16[128,129]{1,0:T(8,128)(2,1)S(1)} %pad_maximum_fusion.2), channel_id=1, replica_groups=mesh['z'=8,'x'=4,'y'=4,'core'=2] {'y','core'}, dimensions={0}, use_global_device_ids=true | all-gather | bytes 297216 | tf_op jit(solution)/shard_map/all_gather | solution.py:167
  39.3 1.2 fusion.5
  40.5 1.1 copy.110.rb_ref
  41.6 1.1 copy.111.ra_ref
  42.7 1.3 dynamic-slice.8
  44.0 1.3 dynamic-slice.7
  46.8 0.9 pad_maximum_fusion.1.qa_ref
  47.6 19.8 %all-gather.6.cloned.1.call-done = bf16[8192,67]{1,0:T(8,128)(2,1)} async-done(((bf16[1024,67]{1,0:T(8,128)(2,1)}), bf16[8192,67]{1,0:T(8,128)(2,1)}) %all-gather.6.cloned.1.call-update) | async-done | bytes 1097744 | tf_op jit(solution)/shard_map/all_gather | solution.py:21
  67.5 3.5 %fusion.21 = (bf16[8192,64]{1,0:T(8,128)(2,1)}, bf16[64,8192]{0,1:T(8,128)(2,1)S(1)}) fusion(bf16[8192,67]{1,0:T(8,128)(2,1)} %all-gather.6.cloned.1.call-done), kind=kLoop, calls=%fused_computation.67 | loop fusion | bytes 3145728 | tf_op jit(solution)/shard_map/slice | solution.py:177
  71.0 2.5 pad_maximum_fusion
  73.5 4.1 %copy.109.yat_ref = bf16[128,8192]{1,0:T(8,128)(2,1)} copy(bf16[128,8192]{0,1:T(8,128)(2,1)} %pad_maximum_fusion) | data formatting | bytes 4194304 | tf_op jit(solution)/shard_map/concatenate | solution.py:192
  77.6 2.4 fusion.1
  80.6 5.0 %convert_reduce_fusion.1 = (f32[]{:T(128)}, f32[]{:T(128)}, f32[8192]{0:T(1024)S(1)}, f32[8192]{0:T(1024)S(1)}) fusion(bf16[8192,67]{1,0:T(8,128)(2,1)S(1)} %copy-done), kind=kLoop, calls=%fused_computation.9 | loop fusion | flops 49150 | bytes 114696 | tf_op jit(solution)/shard_map/reduce_sum | solution.py:180
  86.3 17.1 %shard_map.103 = f32[1024,1]{1,0:T(8,128)} custom-call(bf16[1024,128]{1,0:T(8,128)(2,1)} %pad_maximum_fusion.1.qa_ref, bf16[128,8192]{1,0:T(8,128)(2,1)} %copy.109.yat_ref, f32[1024,1]{1,0:T(8,128)} %copy.110.rb_ref, f32[1,8192]{1,0:T(1,128)} %bitcast.25, f32[1024,1]{1,0:T(8,128)} %copy.111.ra_ref, f32[1,8192]{1,0:T(1,128)} %add_add_fusion.ca_ref), custom_call_target="tpu_custom_call" | custom-call | tf_op jit(solution)/shard_map/pallas_call | solution.py:55
  103.4 1.4 reduce.9
  104.8 1.3 concatenate.28
  106.3 3.3 %all-reduce.1 = f32[2052]{0:T(1024)S(1)} all-reduce(f32[2052]{0:T(1024)S(1)} %dynamic-update-slice.3), channel_id=2, replica_groups=mesh['z'=8,'x'=4,'y'=4,'core'=2] {'core'}, use_global_device_ids=true, to_apply=%add.1 | all-reduce | flops 2052 | bytes 16416
  109.9 17.0 %all-reduce.2 = f32[4104]{0:T(1024)S(1)} all-reduce(f32[4104]{0:T(1024)S(1)} %maximum_dynamic-update-slice_fusion), channel_id=3, replica_groups=mesh['z'=8,'x'=4,'y'=4,'core'=2] {'y'}, use_global_device_ids=true, to_apply=%add.2 | all-reduce | flops 4104 | bytes 32832
  130.0 1.0 log_add_fusion.ra_ref
  131.0 17.6 %shard_map.104 = f32[1,8192]{1,0:T(1,128)} custom-call(bf16[1024,128]{1,0:T(8,128)(2,1)} %pad_maximum_fusion.1.qa_ref, bf16[128,8192]{1,0:T(8,128)(2,1)} %copy.109.yat_ref, f32[1024,1]{1,0:T(8,128)} %copy.110.rb_ref, f32[1,8192]{1,0:T(1,128)} %bitcast.26, f32[1024,1]{1,0:T(8,128)} %log_add_fusion.ra_ref, f32[1,8192]{1,0:T(1,128)} %bitcast.29), custom_call_target="tpu_custom_call" | custom-call | tf_op jit(solution)/shard_map/pallas_call | solution.py:99
  148.6 12.2 %all-gather.3 = f32[4,1,8192]{2,1,0:T(1,128)S(1)} all-gather(f32[1,1,8192]{2,1,0:T(1,128)} %bitcast.33), channel_id=1, replica_groups=mesh['z'=8,'x'=4,'y'=4,'core'=2] {'x'}, dimensions={0}, use_global_device_ids=true | all-gather | bytes 163840 | tf_op jit(solution)/shard_map/all_gather | solution.py:216
  161.1 24.8 %all-gather.2 = f32[65536]{0:T(1024)S(1)} all-gather(f32[8192]{0:T(1024)S(1)} %log_add_fusion.1), channel_id=4, replica_groups=mesh['z'=8,'x'=4,'y'=4,'core'=2] {'z'}, dimensions={0}, use_global_device_ids=true | all-gather | bytes 294912 | tf_op jit(solution)/shard_map/all_gather | solution.py:217
  187.4 4.7 %maximum_maximum_fusion.f_ref = bf16[8192,256]{1,0:T(8,128)(2,1)} fusion(bf16[8192,64]{1,0:T(8,128)(2,1)} %get-tuple-element.46, bf16[8192,64]{1,0:T(8,128)(2,1)S(1)} %copy-done.1, bf16[256]{0:T(256)(128)(2,1)S(1)} %pad.6.clone, bf16[256]{0:T(256)(128)(2,1)S(1)} %pad.5.clone), kind=kLoop, calls=%fused_computation.8 | loop fusion | flops 16777216 | bytes 6292480 | tf_op jit(solution)/shard_map/concatenate | solution.py:194
  192.1 16.5 %shard_map.105 = f32[1024,256]{1,0:T(8,128)} custom-call(bf16[1024,128]{1,0:T(8,128)(2,1)} %pad_maximum_fusion.1.qa_ref, bf16[128,8192]{1,0:T(8,128)(2,1)} %copy.109.yat_ref, f32[1024,1]{1,0:T(8,128)} %copy.110.rb_ref, f32[1,8192]{1,0:T(1,128)} %bitcast.27, f32[1024,1]{1,0:T(8,128)} %copy-done.2, f32[1,8192]{1,0:T(1,128)} %add_subtract_fusion.ca_ref, ...), custom_call_target="tpu_custom_call" | custom-call | tf_op jit(solution)/shard_map/pallas_call | solution.py:140
  208.7 31.7 %reduce-scatter.2.cloned.1.call-done = f32[128,129]{1,0:T(8,128)} async-done(((f32[1024,129]{1,0:T(8,128)}), f32[128,129]{1,0:T(8,128)}) %reduce-scatter.2.cloned.1.call-update) | async-done | bytes 66064 | tf_op jit(solution)/shard_map/reduce_scatter | solution.py:224
  240.4 0.9 slice_reduce_fusion
  241.3 1.0 fusion.13
  (54 shorter events, 8.0 us)
Async XLA Ops:
  7.2 60.3 %all-gather.6.cloned.1.call-start = ((), (), s32[]{:S(2)}) async-start(), calls=%async_computation.1 | async-start | bytes 2359296 | tf_op jit(solution)/shard_map/all_gather | solution.py:21
  23.8 216.5 %reduce-scatter.2.cloned.1.call-start = ((), (), s32[]{:S(2)}) async-start(), calls=%async_computation.2 | async-start | bytes 1179648 | tf_op jit(solution)/shard_map/reduce_scatter | solution.py:224
  71.0 6.6 %copy-start = (bf16[8192,67]{1,0:T(8,128)(2,1)S(1)}, bf16[8192,67]{1,0:T(8,128)(2,1)}, u32[]{:S(2)}) copy-start(bf16[8192,67]{1,0:T(8,128)(2,1)} %all-gather.6.cloned.1.call-done) | copy-start | bytes 3293188
  71.0 6.6 %copy-start.5 = (f32[64]{0:T(128)S(1)}, f32[64]{0:T(128)}, u32[]{:S(2)}) copy-start(f32[64]{0:T(128)} %param.16) | copy-start | bytes 772
  80.6 22.8 %copy-start.3 = (f32[8192]{0:T(1024)}, f32[8192]{0:T(1024)S(1)}, u32[]{:S(2)}) copy-start(f32[8192]{0:T(1024)S(1)} %get-tuple-element.55) | copy-start | bytes 98308
  103.4 84.1 %copy-start.1 = (bf16[8192,64]{1,0:T(8,128)(2,1)S(1)}, bf16[8192,64]{1,0:T(8,128)(2,1)}, u32[]{:S(2)}) copy-start(bf16[8192,64]{1,0:T(8,128)(2,1)} %get-tuple-element.44) | copy-start | bytes 3145732
  104.8 82.0 %copy-start.4 = (f32[8192]{0:T(1024)S(1)}, f32[8192]{0:T(1024)}, u32[]{:S(2)}) copy-start(f32[8192]{0:T(1024)} %copy-done.3) | copy-start | bytes 98308
  130.0 62.2 %copy-start.2 = (f32[1024,1]{1,0:T(8,128)}, f32[1024,1]{1,0:T(8,128)S(1)}, u32[]{:S(2)}) copy-start(f32[1024,1]{1,0:T(8,128)S(1)} %copy.113.ra_ref) | copy-start | bytes 12292
  192.1 49.2 %copy-start.6 = (f32[64]{0:T(128)S(1)}, f32[64]{0:T(128)}, u32[]{:S(2)}) copy-start(f32[64]{0:T(128)} %param.17) | copy-start | bytes 772
Sparse Core Ops, SparseCore 0:
  24.0 43.4 all-gather.5
  208.8 31.5 reduce-scatter.1

commit v8 on v7

--- a/solution.py
+++ b/solution.py
@@ -19,6 +19,11 @@
 def gather_row(value):
     inner = lax.all_gather(value, ROW[1], axis=0, tiled=True)
     return lax.all_gather(inner, ROW[0], axis=0, tiled=True)
+
+
+def gather_col(value):
+    inner = lax.all_gather(value, COL[1], axis=0, tiled=True)
+    return lax.all_gather(inner, COL[0], axis=0, tiled=True)
 
 
 KF = 256
@@ -203,9 +208,7 @@
     row_local = row_lse(q_core, y_core_t, row_basket2, col_basket2, row_term2, gshift)
     nu_part = jnp.sum(mass_cols)
     row_msg = jnp.concatenate([row_local, jnp.stack([nu_part, rmass_part])])
-    row_core = lax.all_gather(row_msg, COL[1], axis=0)
-    row_msg = jnp.concatenate([merge_lse(row_core[:, :nrows]), jnp.sum(row_core[:, nrows:], axis=0)])
-    row_all = lax.all_gather(row_msg, COL[0], axis=0)
+    row_all = gather_col(row_msg[None, :])
     nu_total = jnp.sum(row_all[:, nrows])
     mu_total = jnp.sum(row_all[:, nrows + 1])
     log_nu_total = jnp.log(nu_total)

time: 251 us -> 247 us (0.984)
  blocking collectives: 84.2 us -> 79.7 us
  waiting for transfers between devices: 51.6 us -> 54.3 us
    unnamed x2 -> x1, blocking collectives: 20.3 us -> 3.28 us
    all_gather x0 -> x1, blocking collectives: none -> 12.6 us  [gather_col(): return lax.all_gather(inner, COL[0], axis=0, tiled=True)]
  transfers between devices with their start and end apart: 2 -> 2, of which waited for: 2 -> 2; matrix products, arithmetic and copies ran while one was open for 4% -> 3% of each run, Pallas kernels for 0% -> 0%
where the time goes in v8:
time: 247 us; the launch traced here: 246 us
  blocking collectives  79.7 us (32%)
  waiting for transfers between devices  54.3 us (22%)
  Pallas kernels  51.2 us (21%)
  other arithmetic  24.8 us (10%)
  local copies, waits for them, and re-layouts  19.6 us (8%)
  between operations  16.3 us (7%)
    reduce_scatter x1, waiting for transfers between devices, sweep(): own = lax.psum_scatter(both, COL, scatter_dimension=0, tiled=True)  32.6 us
    all_gather x1, blocking collectives, sweep(): col_all = lax.all_gather(col_x, ROW[0], axis=0)  24.8 us
    all_gather x1, waiting for transfers between devices, gather_row(): return lax.all_gather(inner, ROW[0], axis=0, tiled=True)  21.8 us
    pallas_call x1, Pallas kernels, col_lse(): pl.pallas_call(functools.partial(_col_lse_kernel, tm=tm), grid=(n // tn,)...  17.6 us
    pallas_call x1, Pallas kernels, row_lse(): pl.pallas_call(functools.partial(_row_lse_kernel, tn=tn), grid=(nr // tm,...  17.1 us
    pallas_call x1, Pallas kernels, moments(): pl.pallas_call(functools.partial(_moment_kernel, tn=tn), grid=(nr // tm,)...  16.5 us
    all_gather x1, blocking collectives, sweep(): x_rows_pack = lax.all_gather(x_pack, COL, axis=0, tiled=True)  13.6 us
    all_gather x1, blocking collectives, gather_row(): inner = lax.all_gather(value, ROW[1], axis=0, tiled=True)  13.3 us
  transfers between devices with their start and end apart: 2, of which 2 were waited for; matrix products, arithmetic and copies ran while one was open for 3% of the time, Pallas kernels for 0%

profile of v8, /device:TPU:2, one launch (start us, length us, event | category | flops | bytes accessed | tf_op | source)
XLA Modules:
  0.0 245.9 jit_solution(18074259864135171544)
XLA Ops:
  7.2 0.8 copy.81
  8.8 0.8 broadcast_in_dim.18
  9.5 0.9 copy.83
  10.5 13.3 %all_gather.23 = bf16[1024,67]{1,0:T(8,128)(2,1)} all-gather(bf16[256,67]{1,0:T(8,128)(2,1)S(1)} %fusion.20), channel_id=1, replica_groups=mesh['z'=8,'x'=4,'y'=4,'core'=2] {'x'}, dimensions={0}, use_global_device_ids=true | all-gather | bytes 171520 | tf_op jit(solution)/shard_map/all_gather | solution.py:20
  23.9 0.8 copy.80
  24.7 0.8 copy.79
  25.7 13.6 %all_gather.22 = bf16[1024,129]{1,0:T(8,128)(2,1)S(1)} all-gather(bf16[128,129]{1,0:T(8,128)(2,1)S(1)} %pad_maximum_fusion.2), channel_id=1, replica_groups=mesh['z'=8,'x'=4,'y'=4,'core'=2] {'y','core'}, dimensions={0}, use_global_device_ids=true | all-gather | bytes 297216 | tf_op jit(solution)/shard_map/all_gather | solution.py:172
  39.3 1.2 fusion.5
  40.5 1.1 copy.87.rb_ref
  41.6 1.1 copy.88.ra_ref
  42.8 1.3 dynamic-slice.7
  44.9 0.9 pad_maximum_fusion.1.qa_ref
  45.7 21.8 %all-gather.6.cloned.1.call-done = bf16[8192,67]{1,0:T(8,128)(2,1)} async-done(((bf16[1024,67]{1,0:T(8,128)(2,1)}), bf16[8192,67]{1,0:T(8,128)(2,1)}) %all-gather.6.cloned.1.call-update) | async-done | bytes 1097744 | tf_op jit(solution)/shard_map/all_gather | solution.py:21
  67.5 3.5 %fusion.21 = (bf16[8192,64]{1,0:T(8,128)(2,1)}, bf16[64,8192]{0,1:T(8,128)(2,1)S(1)}) fusion(bf16[8192,67]{1,0:T(8,128)(2,1)} %all-gather.6.cloned.1.call-done), kind=kLoop, calls=%fused_computation.62 | loop fusion | bytes 3145728 | tf_op jit(solution)/shard_map/slice | solution.py:182
  71.0 2.5 %pad_maximum_fusion = bf16[128,8192]{0,1:T(8,128)(2,1)} fusion(bf16[64,8192]{0,1:T(8,128)(2,1)S(1)} %get-tuple-element.42), kind=kLoop, calls=%fused_computation.11 | loop fusion | flops 4194304 | bytes 3145728 | tf_op jit(solution)/shard_map/concatenate | solution.py:197
  73.5 4.1 %copy.86.yat_ref = bf16[128,8192]{1,0:T(8,128)(2,1)} copy(bf16[128,8192]{0,1:T(8,128)(2,1)} %pad_maximum_fusion) | data formatting | bytes 4194304 | tf_op jit(solution)/shard_map/concatenate | solution.py:197
  77.6 2.4 fusion.1
  80.6 5.0 %convert_reduce_fusion.1 = (f32[]{:T(128)}, f32[]{:T(128)}, f32[8192]{0:T(1024)S(1)}, f32[8192]{0:T(1024)S(1)}) fusion(bf16[8192,67]{1,0:T(8,128)(2,1)S(1)} %copy-done), kind=kLoop, calls=%fused_computation.9 | loop fusion | flops 49150 | bytes 114696 | tf_op jit(solution)/shard_map/reduce_sum | solution.py:185
  86.2 17.1 %shard_map.103 = f32[1024,1]{1,0:T(8,128)} custom-call(bf16[1024,128]{1,0:T(8,128)(2,1)} %pad_maximum_fusion.1.qa_ref, bf16[128,8192]{1,0:T(8,128)(2,1)} %copy.86.yat_ref, f32[1024,1]{1,0:T(8,128)} %copy.87.rb_ref, f32[1,8192]{1,0:T(1,128)} %bitcast.24, f32[1024,1]{1,0:T(8,128)} %copy.88.ra_ref, f32[1,8192]{1,0:T(1,128)} %add_add_fusion.ca_ref), custom_call_target="tpu_custom_call" | custom-call | tf_op jit(solution)/shard_map/pallas_call | solution.py:60
  103.3 1.4 reduce.9
  104.7 1.3 concatenate.25
  106.3 3.3 %all-reduce.1 = f32[2052]{0:T(1024)S(1)} all-reduce(f32[2052]{0:T(1024)S(1)} %dynamic-update-slice.3), channel_id=2, replica_groups=mesh['z'=8,'x'=4,'y'=4,'core'=2] {'core'}, use_global_device_ids=true, to_apply=%add.1 | all-reduce | flops 2052 | bytes 16416
  109.6 12.6 %all-gather.2 = f32[4,2,1026]{2,1,0:T(2,128)S(1)} all-gather(f32[1,2,1026]{2,1,0:T(2,128)S(1)} %reshape.237), channel_id=1, replica_groups=mesh['z'=8,'x'=4,'y'=4,'core'=2] {'y'}, dimensions={0}, use_global_device_ids=true | all-gather | bytes 41040 | tf_op jit(solution)/shard_map/all_gather | solution.py:26
  125.2 1.0 log_add_fusion.ra_ref
  126.3 17.6 %shard_map.104 = f32[1,8192]{1,0:T(1,128)} custom-call(bf16[1024,128]{1,0:T(8,128)(2,1)} %pad_maximum_fusion.1.qa_ref, bf16[128,8192]{1,0:T(8,128)(2,1)} %copy.86.yat_ref, f32[1024,1]{1,0:T(8,128)} %copy.87.rb_ref, f32[1,8192]{1,0:T(1,128)} %bitcast.25, f32[1024,1]{1,0:T(8,128)} %log_add_fusion.ra_ref, f32[1,8192]{1,0:T(1,128)} %bitcast.28), custom_call_target="tpu_custom_call" | custom-call | tf_op jit(solution)/shard_map/pallas_call | solution.py:104
  143.8 12.1 %all-gather.3 = f32[4,1,8192]{2,1,0:T(1,128)S(1)} all-gather(f32[1,1,8192]{2,1,0:T(1,128)} %bitcast.32), channel_id=1, replica_groups=mesh['z'=8,'x'=4,'y'=4,'core'=2] {'x'}, dimensions={0}, use_global_device_ids=true | all-gather | bytes 163840 | tf_op jit(solution)/shard_map/all_gather | solution.py:219
  156.3 24.8 %all-gather.1 = f32[65536]{0:T(1024)S(1)} all-gather(f32[8192]{0:T(1024)S(1)} %log_add_fusion.1), channel_id=3, replica_groups=mesh['z'=8,'x'=4,'y'=4,'core'=2] {'z'}, dimensions={0}, use_global_device_ids=true | all-gather | bytes 294912 | tf_op jit(solution)/shard_map/all_gather | solution.py:220
  182.6 4.7 %maximum_maximum_fusion.f_ref = bf16[8192,256]{1,0:T(8,128)(2,1)} fusion(bf16[8192,64]{1,0:T(8,128)(2,1)} %get-tuple-element.43, bf16[8192,64]{1,0:T(8,128)(2,1)S(1)} %copy-done.1, bf16[256]{0:T(256)(128)(2,1)S(1)} %pad.6.clone, bf16[256]{0:T(256)(128)(2,1)S(1)} %pad.5.clone), kind=kLoop, calls=%fused_computation.8 | loop fusion | flops 16777216 | bytes 6292480 | tf_op jit(solution)/shard_map/concatenate | solution.py:199
  187.3 16.5 %shard_map.105 = f32[1024,256]{1,0:T(8,128)} custom-call(bf16[1024,128]{1,0:T(8,128)(2,1)} %pad_maximum_fusion.1.qa_ref, bf16[128,8192]{1,0:T(8,128)(2,1)} %copy.86.yat_ref, f32[1024,1]{1,0:T(8,128)} %copy.87.rb_ref, f32[1,8192]{1,0:T(1,128)} %bitcast.26, f32[1024,1]{1,0:T(8,128)} %copy-done.2, f32[1,8192]{1,0:T(1,128)} %add_subtract_fusion.ca_ref, ...), custom_call_target="tpu_custom_call" | custom-call | tf_op jit(solution)/shard_map/pallas_call | solution.py:145
  203.9 32.6 %reduce-scatter.2.cloned.1.call-done = f32[128,129]{1,0:T(8,128)} async-done(((f32[1024,129]{1,0:T(8,128)}), f32[128,129]{1,0:T(8,128)}) %reduce-scatter.2.cloned.1.call-update) | async-done | bytes 66064 | tf_op jit(solution)/shard_map/reduce_scatter | solution.py:227
  236.4 0.9 slice_reduce_fusion
  237.4 1.0 fusion.13
  (47 shorter events, 7.0 us)
Async XLA Ops:
  7.2 60.3 %all-gather.6.cloned.1.call-start = ((), (), s32[]{:S(2)}) async-start(), calls=%async_computation.1 | async-start | bytes 2359296 | tf_op jit(solution)/shard_map/all_gather | solution.py:21
  23.8 212.6 %reduce-scatter.2.cloned.1.call-start = ((), (), s32[]{:S(2)}) async-start(), calls=%async_computation.2 | async-start | bytes 1179648 | tf_op jit(solution)/shard_map/reduce_scatter | solution.py:227
  71.0 6.6 %copy-start = (bf16[8192,67]{1,0:T(8,128)(2,1)S(1)}, bf16[8192,67]{1,0:T(8,128)(2,1)}, u32[]{:S(2)}) copy-start(bf16[8192,67]{1,0:T(8,128)(2,1)} %all-gather.6.cloned.1.call-done) | copy-start | bytes 3293188
  71.0 6.6 %copy-start.5 = (f32[64]{0:T(128)S(1)}, f32[64]{0:T(128)}, u32[]{:S(2)}) copy-start(f32[64]{0:T(128)} %param.16) | copy-start | bytes 772
  80.6 22.7 %copy-start.3 = (f32[8192]{0:T(1024)}, f32[8192]{0:T(1024)S(1)}, u32[]{:S(2)}) copy-start(f32[8192]{0:T(1024)S(1)} %get-tuple-element.52) | copy-start | bytes 98308
  103.3 79.3 %copy-start.1 = (bf16[8192,64]{1,0:T(8,128)(2,1)S(1)}, bf16[8192,64]{1,0:T(8,128)(2,1)}, u32[]{:S(2)}) copy-start(bf16[8192,64]{1,0:T(8,128)(2,1)} %get-tuple-element.41) | copy-start | bytes 3145732
  104.7 77.3 %copy-start.4 = (f32[8192]{0:T(1024)S(1)}, f32[8192]{0:T(1024)}, u32[]{:S(2)}) copy-start(f32[8192]{0:T(1024)} %copy-done.3) | copy-start | bytes 98308
  125.2 62.1 %copy-start.2 = (f32[1024,1]{1,0:T(8,128)}, f32[1024,1]{1,0:T(8,128)S(1)}, u32[]{:S(2)}) copy-start(f32[1024,1]{1,0:T(8,128)S(1)} %copy.89.ra_ref) | copy-start | bytes 12292
  187.3 50.1 %copy-start.6 = (f32[64]{0:T(128)S(1)}, f32[64]{0:T(128)}, u32[]{:S(2)}) copy-start(f32[64]{0:T(128)} %param.17) | copy-start | bytes 772
Sparse Core Ops, SparseCore 0:
  24.0 43.4 all-gather.5
  204.0 32.3 reduce-scatter.1

commit v9 on v8

--- a/solution.py
+++ b/solution.py
@@ -26,13 +26,13 @@
     return lax.all_gather(inner, COL[0], axis=0, tiled=True)
 
 
-KF = 256
+KF = 129
 INTERPRET = False
 
 
 def _row_lse_kernel(qa_ref, yat_ref, rb_ref, cb_ref, ra_ref, ca_ref, out_ref, *, tn):
     tm = qa_ref.shape[0]
-    n = yat_ref.shape[1]
+    n = yat_ref.shape[0]
     qa = qa_ref[...]
     rb = rb_ref[...]
     ra = ra_ref[...]
@@ -40,7 +40,7 @@
     def body(k, carry):
         m, l = carry
         j = pl.multiple_of(k * tn, tn)
-        s = jnp.dot(qa, yat_ref[:, pl.ds(j, tn)], preferred_element_type=jnp.float32)
+        s = lax.dot_general(qa, yat_ref[pl.ds(j, tn), :], (((1,), (1,)), ((), ())), preferred_element_type=jnp.float32)
         z = s + ra + ca_ref[:, pl.ds(j, tn)] + jnp.maximum(cb_ref[:, pl.ds(j, tn)] - rb, 0.0)
         m_new = jnp.maximum(m, jnp.max(z, axis=1, keepdims=True))
         l = l * jnp.exp(m - m_new) + jnp.sum(jnp.exp(z - m_new), axis=1, keepdims=True)
@@ -54,7 +54,7 @@
 
 def row_lse(qa, yat, rb, cb, ra, ca, tm=512, tn=2048):
     nr, kq = qa.shape
-    n = yat.shape[1]
+    n = yat.shape[0]
     tm = min(tm, nr)
     tn = min(tn, n)
     return pl.pallas_call(
@@ -62,7 +62,7 @@
         grid=(nr // tm,),
         in_specs=[
             pl.BlockSpec((tm, kq), lambda i: (i, 0)),
-            pl.BlockSpec((kq, n), lambda i: (0, 0)),
+            pl.BlockSpec((n, kq), lambda i: (0, 0)),
             pl.BlockSpec((tm, 1), lambda i: (i, 0)),
             pl.BlockSpec((1, n), lambda i: (0, 0)),
             pl.BlockSpec((tm, 1), lambda i: (i, 0)),
@@ -75,7 +75,7 @@
 
 
 def _col_lse_kernel(qa_ref, yat_ref, rb_ref, cb_ref, ra_ref, ca_ref, out_ref, *, tm):
-    tn = yat_ref.shape[1]
+    tn = yat_ref.shape[0]
     nr = qa_ref.shape[0]
     yat = yat_ref[...]
     cb = cb_ref[...]
@@ -84,7 +84,7 @@
     def body(k, carry):
         m, l = carry
         i = pl.multiple_of(k * tm, tm)
-        s = jnp.dot(qa_ref[pl.ds(i, tm), :], yat, preferred_element_type=jnp.float32)
+        s = lax.dot_general(qa_ref[pl.ds(i, tm), :], yat, (((1,), (1,)), ((), ())), preferred_element_type=jnp.float32)
         z = s + ra_ref[pl.ds(i, tm), :] + ca + jnp.maximum(cb - rb_ref[pl.ds(i, tm), :], 0.0)
         m_new = jnp.maximum(m, jnp.max(z, axis=0, keepdims=True))
         l = l * jnp.exp(m - m_new) + jnp.sum(jnp.exp(z - m_new), axis=0, keepdims=True)
@@ -98,7 +98,7 @@
 
 def col_lse(qa, yat, rb, cb, ra, ca, tm=512, tn=1024):
     nr, kq = qa.shape
-    n = yat.shape[1]
+    n = yat.shape[0]
     tm = min(tm, nr)
     tn = min(tn, n)
     return pl.pallas_call(
@@ -106,7 +106,7 @@
         grid=(n // tn,),
         in_specs=[
             pl.BlockSpec((nr, kq), lambda j: (0, 0)),
-            pl.BlockSpec((kq, tn), lambda j: (0, j)),
+            pl.BlockSpec((tn, kq), lambda j: (j, 0)),
             pl.BlockSpec((nr, 1), lambda j: (0, 0)),
             pl.BlockSpec((1, tn), lambda j: (0, j)),
             pl.BlockSpec((nr, 1), lambda j: (0, 0)),
@@ -120,14 +120,14 @@
 
 def _moment_kernel(qa_ref, yat_ref, rb_ref, cb_ref, ra_ref, ca_ref, f_ref, out_ref, *, tn):
     tm = qa_ref.shape[0]
-    n = yat_ref.shape[1]
+    n = yat_ref.shape[0]
     qa = qa_ref[...]
     rb = rb_ref[...]
     ra = ra_ref[...]
 
     def body(k, acc):
         j = pl.multiple_of(k * tn, tn)
-        s = jnp.dot(qa, yat_ref[:, pl.ds(j, tn)], preferred_element_type=jnp.float32)
+        s = lax.dot_general(qa, yat_ref[pl.ds(j, tn), :], (((1,), (1,)), ((), ())), preferred_element_type=jnp.float32)
         z = s + ra + ca_ref[:, pl.ds(j, tn)] + jnp.maximum(cb_ref[:, pl.ds(j, tn)] - rb, 0.0)
         plan = jnp.exp(z).astype(jnp.bfloat16)
         return acc + jnp.dot(plan, f_ref[pl.ds(j, tn), :], preferred_element_type=jnp.float32)
@@ -138,7 +138,7 @@
 
 def moments(qa, yat, rb, cb, ra, ca, feats, tm=512, tn=2048):
     nr, kq = qa.shape
-    n = yat.shape[1]
+    n = yat.shape[0]
     tm = min(tm, nr)
     tn = min(tn, n)
     nf = feats.shape[1]
@@ -147,7 +147,7 @@
         grid=(nr // tm,),
         in_specs=[
             pl.BlockSpec((tm, kq), lambda i: (i, 0)),
-            pl.BlockSpec((kq, n), lambda i: (0, 0)),
+            pl.BlockSpec((n, kq), lambda i: (0, 0)),
             pl.BlockSpec((tm, 1), lambda i: (i, 0)),
             pl.BlockSpec((1, n), lambda i: (0, 0)),
             pl.BlockSpec((tm, 1), lambda i: (i, 0)),
@@ -191,10 +191,10 @@
     q_core = jnp.concatenate([mult_rows * 2, x_rows * (2.0 * KAPPA / width * 2.0)], axis=1)
     log_row = jnp.log(mass_rows.astype(jnp.float32))
     yf = y_cols.astype(jnp.float32)
-    col_term2 = 2.0 * (-(KAPPA / width) * jnp.sum(yf * yf, axis=1))
-    col_basket2 = 2.0 * jnp.sum(yf * basket[None, :], axis=1)
-    y_t = y_cols.T
-    y_core_t = jnp.concatenate([y_t, y_t], axis=0)
+    hi = lax.Precision.HIGHEST
+    col_term2 = 2.0 * (-(KAPPA / width) * jnp.dot(yf * yf, jnp.ones((width,), jnp.float32), precision=hi))
+    col_basket2 = 2.0 * jnp.dot(yf, basket, precision=hi)
+    y_core_t = jnp.concatenate([y_cols, y_cols], axis=1)
     ny_cols = y_cols.shape[0]
     features = jnp.concatenate(
         [yf, yf * yf, jnp.ones((ny_cols, 1), jnp.float32),

time: 247 us -> 243 us (0.984)
  local copies, waits for them, and re-layouts: 19.6 us -> 11.9 us
  matrix products: 0 us -> 7.41 us
    dot_general x0 -> x2, matrix products: none -> 7.41 us  [the longest x1 3.95 us: sweep(): jnp.dot(yf * yf, jnp.ones((width,), jnp.float32), precision=hi)]
    concatenate x1 -> x0, local copies, waits for them, and re-layouts: 4.12 us -> none  [sweep(): y_core_t = jnp.concatenate([y_t, y_t], axis=0)]
    slice x1 -> x0, local copies, waits for them, and re-layouts: 3.48 us -> none  [sweep(): y_cols = y_cols_pack[:, :width]]
where the time goes in v9:
time: 243 us
  blocking collectives  79.6 us (33%)
  waiting for transfers between devices  54.6 us (22%)
  Pallas kernels  50.1 us (21%)
  other arithmetic  22.8 us (9%)
  between operations  16.2 us (7%)
  local copies, waits for them, and re-layouts  11.9 us (5%)
  matrix products  7.41 us (3%)
    reduce_scatter x1, waiting for transfers between devices, sweep(): own = lax.psum_scatter(both, COL, scatter_dimension=0, tiled=True)  32.6 us
    all_gather x1, blocking collectives, sweep(): col_all = lax.all_gather(col_x, ROW[0], axis=0)  24.8 us
    all_gather x1, waiting for transfers between devices, gather_row(): return lax.all_gather(inner, ROW[0], axis=0, tiled=True)  21.9 us
    pallas_call x1, Pallas kernels, col_lse(): pl.pallas_call(functools.partial(_col_lse_kernel, tm=tm), grid=(n // tn,)...  17.8 us
    pallas_call x1, Pallas kernels, row_lse(): pl.pallas_call(functools.partial(_row_lse_kernel, tn=tn), grid=(nr // tm,...  16.8 us
    pallas_call x1, Pallas kernels, moments(): pl.pallas_call(functools.partial(_moment_kernel, tn=tn), grid=(nr // tm,)...  15.5 us
    all_gather x1, blocking collectives, sweep(): x_rows_pack = lax.all_gather(x_pack, COL, axis=0, tiled=True)  13.6 us
    all_gather x1, blocking collectives, gather_row(): inner = lax.all_gather(value, ROW[1], axis=0, tiled=True)  13.3 us
  transfers between devices with their start and end apart: 2, of which 2 were waited for; matrix products, arithmetic and copies ran while one was open for 3% of the time, Pallas kernels for 0%

profile of v9, /device:TPU:2, one launch (start us, length us, event | category | flops | bytes accessed | tf_op | source)
XLA Modules:
  0.0 242.7 jit_solution(9045525495986049658)
XLA Ops:
  7.2 0.8 copy.69
  8.0 0.9 copy.71
  8.9 0.8 broadcast_in_dim.56
  9.6 0.8 broadcast_in_dim.55
  10.5 13.3 %all_gather.23 = bf16[1024,67]{1,0:T(8,128)(2,1)} all-gather(bf16[256,67]{1,0:T(8,128)(2,1)S(1)} %fusion.19), channel_id=1, replica_groups=mesh['z'=8,'x'=4,'y'=4,'core'=2] {'x'}, dimensions={0}, use_global_device_ids=true | all-gather | bytes 171520 | tf_op jit(solution)/shard_map/all_gather | solution.py:20
  23.9 0.8 copy.67
  24.7 0.8 copy.68
  25.7 13.6 %all_gather.22 = bf16[1024,129]{1,0:T(8,128)(2,1)S(1)} all-gather(bf16[128,129]{1,0:T(8,128)(2,1)S(1)} %pad_maximum_fusion.2), channel_id=1, replica_groups=mesh['z'=8,'x'=4,'y'=4,'core'=2] {'y','core'}, dimensions={0}, use_global_device_ids=true | all-gather | bytes 297216 | tf_op jit(solution)/shard_map/all_gather | solution.py:172
  39.3 1.2 fusion.4
  40.6 1.0 copy.74.rb_ref
  41.6 1.0 copy.75.ra_ref
  42.6 1.3 dynamic-slice.7
  44.7 0.9 pad_maximum_fusion.1.qa_ref
  45.5 21.9 %all-gather.6.cloned.1.call-done = bf16[8192,67]{1,0:T(8,128)(2,1)} async-done(((bf16[1024,67]{1,0:T(8,128)(2,1)}), bf16[8192,67]{1,0:T(8,128)(2,1)}) %all-gather.6.cloned.1.call-update) | async-done | bytes 1097744 | tf_op jit(solution)/shard_map/all_gather | solution.py:21
  67.5 3.5 %fusion.20 = f32[1,8192]{1,0:T(1,128)S(1)} fusion(f32[64]{0:T(128)S(1)} %copy-done.2, bf16[8192,67]{1,0:T(8,128)(2,1)} %all-gather.6.cloned.1.call-done), kind=kOutput, calls=%fused_computation.58 | convolution fusion | flops 6291456 | bytes 1130752 | tf_op jit(solution)/shard_map/dot_general | solution.py:196
  71.6 4.7 %pad_maximum_fusion.yat_ref = bf16[8192,128]{1,0:T(8,128)(2,1)} fusion(bf16[8192,64]{1,0:T(8,128)(2,1)} %bitcast.25), kind=kLoop, calls=%fused_computation.9 | loop fusion | flops 4194304 | bytes 3145728 | tf_op jit(solution)/shard_map/concatenate | solution.py:197
  76.3 4.0 %fusion.2 = f32[1,8192]{1,0:T(1,128)S(1)} fusion(bf16[8192,67]{1,0:T(8,128)(2,1)S(1)} %copy-done), kind=kOutput, calls=%fused_computation.8 | convolution fusion | flops 7340032 | bytes 1130496 | tf_op jit(solution)/shard_map/dot_general | solution.py:195
  80.3 5.1 %convert_reduce_fusion.1 = (f32[]{:T(128)}, f32[]{:T(128)}, f32[8192]{0:T(1024)S(1)}, f32[8192]{0:T(1024)S(1)}) fusion(bf16[8192,67]{1,0:T(8,128)(2,1)S(1)} %copy-done), kind=kLoop, calls=%fused_computation.4 | loop fusion | flops 49150 | bytes 114696 | tf_op jit(solution)/shard_map/reduce_sum | solution.py:185
  86.0 16.8 %shard_map.103 = f32[1024,1]{1,0:T(8,128)} custom-call(bf16[1024,128]{1,0:T(8,128)(2,1)} %pad_maximum_fusion.1.qa_ref, bf16[8192,128]{1,0:T(8,128)(2,1)} %pad_maximum_fusion.yat_ref, f32[1024,1]{1,0:T(8,128)} %copy.74.rb_ref, f32[1,8192]{1,0:T(1,128)} %bitcast.27, f32[1024,1]{1,0:T(8,128)} %copy.75.ra_ref, f32[1,8192]{1,0:T(1,128)} %bitcast.31), custom_call_target="tpu_custom_call" | custom-call | tf_op jit(solution)/shard_map/pallas_call | solution.py:60
  102.8 1.2 reduce.9
  104.0 1.4 concatenate.25
  105.7 3.3 %all-reduce.1 = f32[2052]{0:T(1024)S(1)} all-reduce(f32[2052]{0:T(1024)S(1)} %dynamic-update-slice.3), channel_id=2, replica_groups=mesh['z'=8,'x'=4,'y'=4,'core'=2] {'core'}, use_global_device_ids=true, to_apply=%add.1 | all-reduce | flops 2052 | bytes 16416
  109.0 12.4 %all-gather.2 = f32[4,2,1026]{2,1,0:T(2,128)S(1)} all-gather(f32[1,2,1026]{2,1,0:T(2,128)S(1)} %reshape.139), channel_id=1, replica_groups=mesh['z'=8,'x'=4,'y'=4,'core'=2] {'y'}, dimensions={0}, use_global_device_ids=true | all-gather | bytes 41040 | tf_op jit(solution)/shard_map/all_gather | solution.py:26
  124.5 1.0 log_add_fusion.ra_ref
  125.4 17.8 %shard_map.104 = f32[1,8192]{1,0:T(1,128)} custom-call(bf16[1024,128]{1,0:T(8,128)(2,1)} %pad_maximum_fusion.1.qa_ref, bf16[8192,128]{1,0:T(8,128)(2,1)} %pad_maximum_fusion.yat_ref, f32[1024,1]{1,0:T(8,128)} %copy.74.rb_ref, f32[1,8192]{1,0:T(1,128)} %bitcast.28, f32[1024,1]{1,0:T(8,128)} %log_add_fusion.ra_ref, f32[1,8192]{1,0:T(1,128)} %bitcast.30), custom_call_target="tpu_custom_call" | custom-call | tf_op jit(solution)/shard_map/pallas_call | solution.py:104
  143.2 12.2 %all-gather.3 = f32[4,1,8192]{2,1,0:T(1,128)S(1)} all-gather(f32[1,1,8192]{2,1,0:T(1,128)} %bitcast.32), channel_id=1, replica_groups=mesh['z'=8,'x'=4,'y'=4,'core'=2] {'x'}, dimensions={0}, use_global_device_ids=true | all-gather | bytes 163840 | tf_op jit(solution)/shard_map/all_gather | solution.py:219
  155.8 24.8 %all-gather.1 = f32[65536]{0:T(1024)S(1)} all-gather(f32[8192]{0:T(1024)S(1)} %log_add_fusion.1), channel_id=3, replica_groups=mesh['z'=8,'x'=4,'y'=4,'core'=2] {'z'}, dimensions={0}, use_global_device_ids=true | all-gather | bytes 294912 | tf_op jit(solution)/shard_map/all_gather | solution.py:220
  181.9 3.2 %maximum_maximum_fusion.f_ref = bf16[8192,129]{1,0:T(8,128)(2,1)} fusion(bf16[8192,64]{1,0:T(8,128)(2,1)S(1)} %fusion.1, bf16[8192,64]{1,0:T(8,128)(2,1)S(1)} %bitcast.26, bf16[129]{0:T(256)(128)(2,1)S(1)} %pad.5.clone), kind=kLoop, calls=%fused_computation.3 | loop fusion | flops 6340608 | bytes 4210946 | tf_op jit(solution)/shard_map/concatenate | solution.py:199
  185.1 15.5 %shard_map.105 = f32[1024,129]{1,0:T(8,128)} custom-call(bf16[1024,128]{1,0:T(8,128)(2,1)} %pad_maximum_fusion.1.qa_ref, bf16[8192,128]{1,0:T(8,128)(2,1)} %pad_maximum_fusion.yat_ref, f32[1024,1]{1,0:T(8,128)} %copy.74.rb_ref, f32[1,8192]{1,0:T(1,128)} %bitcast.29, f32[1024,1]{1,0:T(8,128)} %copy-done.1, f32[1,8192]{1,0:T(1,128)} %bitcast.34, ...), custom_call_target="tpu_custom_call" | custom-call | tf_op jit(solution)/shard_map/pallas_call | solution.py:145
  200.6 32.6 %reduce-scatter.2.cloned.1.call-done = f32[128,129]{1,0:T(8,128)} async-done(((f32[1024,129]{1,0:T(8,128)}), f32[128,129]{1,0:T(8,128)}) %reduce-scatter.2.cloned.1.call-update) | async-done | bytes 66064 | tf_op jit(solution)/shard_map/reduce_scatter | solution.py:227
  233.2 0.9 slice_reduce_fusion
  234.1 1.0 fusion.12
  (38 shorter events, 6.0 us)
Async XLA Ops:
  7.2 60.3 %copy-start.2 = (f32[64]{0:T(128)S(1)}, f32[64]{0:T(128)}, u32[]{:S(2)}) copy-start(f32[64]{0:T(128)} %param.16) | copy-start | bytes 772
  7.2 60.3 %all-gather.6.cloned.1.call-start = ((), (), s32[]{:S(2)}) async-start(), calls=%async_computation.1 | async-start | bytes 2359296 | tf_op jit(solution)/shard_map/all_gather | solution.py:21
  23.9 209.3 %reduce-scatter.2.cloned.1.call-start = ((), (), s32[]{:S(2)}) async-start(), calls=%async_computation.2 | async-start | bytes 1179648 | tf_op jit(solution)/shard_map/reduce_scatter | solution.py:227
  67.5 8.8 %copy-start = (bf16[8192,67]{1,0:T(8,128)(2,1)S(1)}, bf16[8192,67]{1,0:T(8,128)(2,1)}, u32[]{:S(2)}) copy-start(bf16[8192,67]{1,0:T(8,128)(2,1)} %all-gather.6.cloned.1.call-done) | copy-start | bytes 3293188
  124.5 57.4 %copy-start.1 = (f32[1024,1]{1,0:T(8,128)}, f32[1024,1]{1,0:T(8,128)S(1)}, u32[]{:S(2)}) copy-start(f32[1024,1]{1,0:T(8,128)S(1)} %copy.76.ra_ref) | copy-start | bytes 12292
  185.1 49.1 %copy-start.3 = (f32[64]{0:T(128)S(1)}, f32[64]{0:T(128)}, u32[]{:S(2)}) copy-start(f32[64]{0:T(128)} %param.17) | copy-start | bytes 772
Sparse Core Ops, SparseCore 0:
  24.0 43.4 all-gather.5
  200.7 32.4 reduce-scatter.1

commit v10 on v9

--- a/solution.py
+++ b/solution.py
@@ -52,7 +52,7 @@
     out_ref[...] = m + jnp.log(l)
 
 
-def row_lse(qa, yat, rb, cb, ra, ca, tm=512, tn=2048):
+def row_lse(qa, yat, rb, cb, ra, ca, tm=1024, tn=2048):
     nr, kq = qa.shape
     n = yat.shape[0]
     tm = min(tm, nr)
@@ -191,9 +191,8 @@
     q_core = jnp.concatenate([mult_rows * 2, x_rows * (2.0 * KAPPA / width * 2.0)], axis=1)
     log_row = jnp.log(mass_rows.astype(jnp.float32))
     yf = y_cols.astype(jnp.float32)
-    hi = lax.Precision.HIGHEST
-    col_term2 = 2.0 * (-(KAPPA / width) * jnp.dot(yf * yf, jnp.ones((width,), jnp.float32), precision=hi))
-    col_basket2 = 2.0 * jnp.dot(yf, basket, precision=hi)
+    col_term2 = 2.0 * (-(KAPPA / width) * jnp.sum(yf * yf, axis=1))
+    col_basket2 = 2.0 * jnp.sum(yf * basket[None, :], axis=1)
     y_core_t = jnp.concatenate([y_cols, y_cols], axis=1)
     ny_cols = y_cols.shape[0]
     features = jnp.concatenate(

time: 243 us -> 239 us (0.984)
  matrix products: 7.41 us -> 0 us
  other arithmetic: 22.8 us -> 26.7 us
    dot_general x2 -> x0, matrix products: 7.41 us -> none  [the longest x1 3.95 us: sweep(): jnp.dot(yf * yf, jnp.ones((width,), jnp.float32), precision=hi)]
    unnamed x17 -> x21, local copies, waits for them, and re-layouts: 4.88 us -> 4.89 us
where the time goes in v10:
time: 239 us
  blocking collectives  79.6 us (33%)
  waiting for transfers between devices  54.5 us (23%)
  Pallas kernels  49.7 us (21%)
  other arithmetic  26.7 us (11%)
  between operations  16.3 us (7%)
  local copies, waits for them, and re-layouts  11.9 us (5%)
    reduce_scatter x1, waiting for transfers between devices, sweep(): own = lax.psum_scatter(both, COL, scatter_dimension=0, tiled=True)  32.5 us
    all_gather x1, blocking collectives, sweep(): col_all = lax.all_gather(col_x, ROW[0], axis=0)  24.8 us
    all_gather x1, waiting for transfers between devices, gather_row(): return lax.all_gather(inner, ROW[0], axis=0, tiled=True)  21.9 us
    pallas_call x1, Pallas kernels, col_lse(): pl.pallas_call(functools.partial(_col_lse_kernel, tm=tm), grid=(n // tn,)...  17.8 us
    pallas_call x1, Pallas kernels, row_lse(): pl.pallas_call(functools.partial(_row_lse_kernel, tn=tn), grid=(nr // tm,...  16.4 us
    pallas_call x1, Pallas kernels, moments(): pl.pallas_call(functools.partial(_moment_kernel, tn=tn), grid=(nr // tm,)...  15.5 us
    all_gather x1, blocking collectives, sweep(): x_rows_pack = lax.all_gather(x_pack, COL, axis=0, tiled=True)  13.6 us
    all_gather x1, blocking collectives, gather_row(): inner = lax.all_gather(value, ROW[1], axis=0, tiled=True)  13.3 us
  transfers between devices with their start and end apart: 2, of which 2 were waited for; matrix products, arithmetic and copies ran while one was open for 3% of the time, Pallas kernels for 0%

profile of v10, /device:TPU:2, one launch (start us, length us, event | category | flops | bytes accessed | tf_op | source)
XLA Modules:
  0.0 238.7 jit_solution(15051957708085991029)
XLA Ops:
  7.2 0.8 copy.69
  8.0 0.9 copy.71
  8.9 0.8 broadcast_in_dim.16
  9.6 0.8 broadcast_in_dim.15
  10.5 13.3 %all_gather.23 = bf16[1024,67]{1,0:T(8,128)(2,1)} all-gather(bf16[256,67]{1,0:T(8,128)(2,1)S(1)} %fusion.20), channel_id=1, replica_groups=mesh['z'=8,'x'=4,'y'=4,'core'=2] {'x'}, dimensions={0}, use_global_device_ids=true | all-gather | bytes 171520 | tf_op jit(solution)/shard_map/all_gather | solution.py:20
  23.9 0.8 copy.67
  24.7 0.8 copy.68
  25.7 13.6 %all_gather.22 = bf16[1024,129]{1,0:T(8,128)(2,1)S(1)} all-gather(bf16[128,129]{1,0:T(8,128)(2,1)S(1)} %pad_maximum_fusion.2), channel_id=1, replica_groups=mesh['z'=8,'x'=4,'y'=4,'core'=2] {'y','core'}, dimensions={0}, use_global_device_ids=true | all-gather | bytes 297216 | tf_op jit(solution)/shard_map/all_gather | solution.py:172
  39.3 1.2 fusion.5
  40.5 1.1 copy.74.rb_ref
  41.6 1.0 copy.75.ra_ref
  42.7 1.3 dynamic-slice.7
  44.7 0.9 pad_maximum_fusion.1.qa_ref
  45.6 21.9 %all-gather.6.cloned.1.call-done = bf16[8192,67]{1,0:T(8,128)(2,1)} async-done(((bf16[1024,67]{1,0:T(8,128)(2,1)}), bf16[8192,67]{1,0:T(8,128)(2,1)}) %all-gather.6.cloned.1.call-update) | async-done | bytes 1097744 | tf_op jit(solution)/shard_map/all_gather | solution.py:21
  67.5 4.9 %pad_maximum_fusion.yat_ref = bf16[8192,128]{1,0:T(8,128)(2,1)} fusion(bf16[8192,64]{1,0:T(8,128)(2,1)} %bitcast.21), kind=kLoop, calls=%fused_computation.11 | loop fusion | flops 4194304 | bytes 3145728 | tf_op jit(solution)/shard_map/concatenate | solution.py:196
  72.3 2.4 fusion.1
  75.3 5.0 %convert_reduce_fusion.1 = (f32[]{:T(128)}, f32[]{:T(128)}, f32[8192]{0:T(1024)S(1)}, f32[8192]{0:T(1024)S(1)}) fusion(bf16[8192,67]{1,0:T(8,128)(2,1)S(1)} %copy-done), kind=kLoop, calls=%fused_computation.9 | loop fusion | flops 49150 | bytes 114696 | tf_op jit(solution)/shard_map/reduce_sum | solution.py:185
  81.0 16.4 %shard_map.103 = f32[1024,1]{1,0:T(8,128)} custom-call(bf16[1024,128]{1,0:T(8,128)(2,1)} %pad_maximum_fusion.1.qa_ref, bf16[8192,128]{1,0:T(8,128)(2,1)} %pad_maximum_fusion.yat_ref, f32[1024,1]{1,0:T(8,128)} %copy.74.rb_ref, f32[1,8192]{1,0:T(1,128)} %bitcast.23, f32[1024,1]{1,0:T(8,128)} %copy.75.ra_ref, f32[1,8192]{1,0:T(1,128)} %add_add_fusion.ca_ref), custom_call_target="tpu_custom_call" | custom-call | tf_op jit(solution)/shard_map/pallas_call | solution.py:60
  97.4 1.2 reduce.9
  98.7 1.3 concatenate.25
  100.3 3.3 %all-reduce.1 = f32[2052]{0:T(1024)S(1)} all-reduce(f32[2052]{0:T(1024)S(1)} %dynamic-update-slice.3), channel_id=2, replica_groups=mesh['z'=8,'x'=4,'y'=4,'core'=2] {'core'}, use_global_device_ids=true, to_apply=%add.1 | all-reduce | flops 2052 | bytes 16416
  103.6 12.5 %all-gather.2 = f32[4,2,1026]{2,1,0:T(2,128)S(1)} all-gather(f32[1,2,1026]{2,1,0:T(2,128)S(1)} %reshape.237), channel_id=1, replica_groups=mesh['z'=8,'x'=4,'y'=4,'core'=2] {'y'}, dimensions={0}, use_global_device_ids=true | all-gather | bytes 41040 | tf_op jit(solution)/shard_map/all_gather | solution.py:26
  119.2 1.0 log_add_fusion.ra_ref
  120.1 17.8 %shard_map.104 = f32[1,8192]{1,0:T(1,128)} custom-call(bf16[1024,128]{1,0:T(8,128)(2,1)} %pad_maximum_fusion.1.qa_ref, bf16[8192,128]{1,0:T(8,128)(2,1)} %pad_maximum_fusion.yat_ref, f32[1024,1]{1,0:T(8,128)} %copy.74.rb_ref, f32[1,8192]{1,0:T(1,128)} %bitcast.24, f32[1024,1]{1,0:T(8,128)} %log_add_fusion.ra_ref, f32[1,8192]{1,0:T(1,128)} %bitcast.27), custom_call_target="tpu_custom_call" | custom-call | tf_op jit(solution)/shard_map/pallas_call | solution.py:104
  137.9 12.1 %all-gather.3 = f32[4,1,8192]{2,1,0:T(1,128)S(1)} all-gather(f32[1,1,8192]{2,1,0:T(1,128)} %bitcast.31), channel_id=1, replica_groups=mesh['z'=8,'x'=4,'y'=4,'core'=2] {'x'}, dimensions={0}, use_global_device_ids=true | all-gather | bytes 163840 | tf_op jit(solution)/shard_map/all_gather | solution.py:218
  150.3 24.8 %all-gather.1 = f32[65536]{0:T(1024)S(1)} all-gather(f32[8192]{0:T(1024)S(1)} %log_add_fusion.1), channel_id=3, replica_groups=mesh['z'=8,'x'=4,'y'=4,'core'=2] {'z'}, dimensions={0}, use_global_device_ids=true | all-gather | bytes 294912 | tf_op jit(solution)/shard_map/all_gather | solution.py:219
  176.7 4.4 %maximum_maximum_fusion.f_ref = bf16[8192,129]{1,0:T(8,128)(2,1)} fusion(bf16[8192,64]{1,0:T(8,128)(2,1)} %get-tuple-element.41, bf16[8192,64]{1,0:T(8,128)(2,1)S(1)} %bitcast.22, bf16[129]{0:T(256)(128)(2,1)S(1)} %pad.5.clone), kind=kLoop, calls=%fused_computation.8 | loop fusion | flops 6340608 | bytes 4210946 | tf_op jit(solution)/shard_map/concatenate | solution.py:198
  181.1 15.5 %shard_map.105 = f32[1024,129]{1,0:T(8,128)} custom-call(bf16[1024,128]{1,0:T(8,128)(2,1)} %pad_maximum_fusion.1.qa_ref, bf16[8192,128]{1,0:T(8,128)(2,1)} %pad_maximum_fusion.yat_ref, f32[1024,1]{1,0:T(8,128)} %copy.74.rb_ref, f32[1,8192]{1,0:T(1,128)} %bitcast.25, f32[1024,1]{1,0:T(8,128)} %copy-done.1, f32[1,8192]{1,0:T(1,128)} %add_subtract_fusion.ca_ref, ...), custom_call_target="tpu_custom_call" | custom-call | tf_op jit(solution)/shard_map/pallas_call | solution.py:145
  196.6 32.5 %reduce-scatter.2.cloned.1.call-done = f32[128,129]{1,0:T(8,128)} async-done(((f32[1024,129]{1,0:T(8,128)}), f32[128,129]{1,0:T(8,128)}) %reduce-scatter.2.cloned.1.call-update) | async-done | bytes 66064 | tf_op jit(solution)/shard_map/reduce_scatter | solution.py:226
  229.2 0.9 slice_reduce_fusion
  230.1 1.0 fusion.13
  231.1 0.7 copy.82
  (41 shorter events, 5.5 us)
Async XLA Ops:
  7.2 60.3 %all-gather.6.cloned.1.call-start = ((), (), s32[]{:S(2)}) async-start(), calls=%async_computation.1 | async-start | bytes 2359296 | tf_op jit(solution)/shard_map/all_gather | solution.py:21
  23.8 205.3 %reduce-scatter.2.cloned.1.call-start = ((), (), s32[]{:S(2)}) async-start(), calls=%async_computation.2 | async-start | bytes 1179648 | tf_op jit(solution)/shard_map/reduce_scatter | solution.py:226
  25.6 46.8 %copy-start.4 = (f32[64]{0:T(128)S(1)}, f32[64]{0:T(128)}, u32[]{:S(2)}) copy-start(f32[64]{0:T(128)} %param.16) | copy-start | bytes 772
  67.5 4.9 %copy-start = (bf16[8192,67]{1,0:T(8,128)(2,1)S(1)}, bf16[8192,67]{1,0:T(8,128)(2,1)}, u32[]{:S(2)}) copy-start(bf16[8192,67]{1,0:T(8,128)(2,1)} %all-gather.6.cloned.1.call-done) | copy-start | bytes 3293188
  75.3 22.1 %copy-start.2 = (f32[8192]{0:T(1024)}, f32[8192]{0:T(1024)S(1)}, u32[]{:S(2)}) copy-start(f32[8192]{0:T(1024)S(1)} %get-tuple-element.50) | copy-start | bytes 98308
  98.7 77.3 %copy-start.3 = (f32[8192]{0:T(1024)S(1)}, f32[8192]{0:T(1024)}, u32[]{:S(2)}) copy-start(f32[8192]{0:T(1024)} %copy-done.2) | copy-start | bytes 98308
  119.1 61.9 %copy-start.1 = (f32[1024,1]{1,0:T(8,128)}, f32[1024,1]{1,0:T(8,128)S(1)}, u32[]{:S(2)}) copy-start(f32[1024,1]{1,0:T(8,128)S(1)} %copy.76.ra_ref) | copy-start | bytes 12292
  181.1 49.0 %copy-start.5 = (f32[64]{0:T(128)S(1)}, f32[64]{0:T(128)}, u32[]{:S(2)}) copy-start(f32[64]{0:T(128)} %param.17) | copy-start | bytes 772
Sparse Core Ops, SparseCore 0:
  24.0 43.4 all-gather.5
  196.7 32.3 reduce-scatter.1
